TPU v7x, 256 devices: a whole 4x4x8 slice. The times are simulated.
256 devices in a mesh: chain: 8 (over x, core), rows: 32 (over z, y).
Axes of the slice: x: 4, y: 4, z: 8, core: 2. Of those that a mesh axis runs over, the one named last changes fastest.
Arguments:
- right_spike: float32 [524288, 256], P(('chain', 'rows')), may hold values from -6 to 6
- left_spike: float32 [524288, 256], P(('chain', 'rows')), may hold values from -6 to 6
- loads: float32 [524288, 256], P(('chain', 'rows')), may hold values from -6 to 6
- tip_inverse: float32 [8, 3, 256, 512], P('chain'), may hold values from -0.0234375 to 0.0234375
Outputs:
- right_final: float32 [524288, 256], P(('chain', 'rows'))
- left_final: float32 [524288, 256], P(('chain', 'rows'))
- loads_final: float32 [524288, 256], P(('chain', 'rows'))
All inputs are finite; a program needn't handle non-finite values.
Results may differ from a plain program's by a relative error of at most 0.00019.
Values sent between devices are 32-bit elements; how exact they have to be, the bound alone decides.
No kernel may reach another device: no remote copies, remote signals or barrier semaphores. Data moves between devices by JAX's collectives and lax.ppermute only.
A program may use at most 64 MiB of HBM per device.

v0:
```python
import jax
import numpy as np
import jax.numpy as jnp
from jax import lax
from jax.experimental import pallas as pl
from jax.experimental.pallas import tpu as pltpu
from jax.sharding import PartitionSpec as P

HALF_BAND = 256
LOAD_COLS = 256
LEVELS = 3


def spread_tips(top, bottom, row_pos, count, fanouts):
    stride = count
    for fanout in fanouts:
        step = stride // fanout
        got_top = top
        got_bottom = bottom
        for k in range(1, fanout):
            offset = k * step
            pairs = [(s, s + offset) for s in range(0, count, stride)]
            pairs += [(s, s - offset) for s in range(stride - 1, count, stride)]
            sent = jnp.where(row_pos % stride == 0, top, bottom)
            got = lax.ppermute(sent, "rows", pairs)
            got_top = jnp.where(row_pos % stride == offset, got, got_top)
            got_bottom = jnp.where(row_pos % stride == stride - 1 - offset, got, got_bottom)
        top = got_top
        bottom = got_bottom
        stride = step
    return top, bottom


def row_fanouts(count):
    fanouts = []
    while count > 1:
        fanout = 4 if count % 4 == 0 else 2
        fanouts.append(fanout)
        count //= fanout
    return fanouts


def bulk_kernel(flag_ref, x_ref, v_ref, w_ref, g_ref, vo_ref, wo_ref, go_ref):
    low = flag_ref[0] == 1
    v = v_ref[...]
    w = w_ref[...]
    driver = jnp.where(low, v, w)
    d_hi = driver.astype(jnp.bfloat16)
    d_lo = (driver - d_hi.astype(jnp.float32)).astype(jnp.bfloat16)
    x = x_ref[...]
    x_hi = x.astype(jnp.bfloat16)
    x_lo = (x - x_hi.astype(jnp.float32)).astype(jnp.bfloat16)
    prod = jnp.dot(d_hi, x_hi, preferred_element_type=jnp.float32)
    prod += jnp.dot(d_hi, x_lo, preferred_element_type=jnp.float32)
    prod += jnp.dot(d_lo, x_hi, preferred_element_type=jnp.float32)
    go_ref[...] = g_ref[...] - prod[:, :LOAD_COLS]
    left_term = prod[:, LOAD_COLS:LOAD_COLS + HALF_BAND]
    right_term = prod[:, LOAD_COLS + HALF_BAND:]
    wo_ref[...] = jnp.where(low, w - left_term, -left_term)
    vo_ref[...] = jnp.where(low, -right_term, v - right_term)


def bulk_update(flag, x, v, w, g, tile=1024):
    rows = v.shape[0]
    block = pl.BlockSpec((tile, HALF_BAND), lambda i, f: (i, 0))
    out = jax.ShapeDtypeStruct((rows, HALF_BAND), jnp.float32)
    return pl.pallas_call(
        bulk_kernel,
        grid_spec=pltpu.PrefetchScalarGridSpec(
            num_scalar_prefetch=1,
            grid=(rows // tile,),
            in_specs=[pl.BlockSpec(x.shape, lambda i, f: (0, 0)), block, block, block],
            out_specs=[block, block, block],
        ),
        out_shape=[out, out, out],
    )(flag, x, v, w, g)


CORE_PLANS = (
    (((2, 0), (4, 0), (6, 0)), ((0, 1), (0, 2), (0, 3)), ((1, 0),)),
    (((0, 1), (0, 2), (0, 3)), ((2, 0), (4, 0), (6, 0)), ((7, 0),)),
)


def core_tree(top, bottom, chain_pos, row_pos, chain_count, z_count, y_count):
    row_count = z_count * y_count
    kinds = len(CORE_PLANS)

    def moved(r, off, sign):
        z, y = divmod(r, y_count)
        return ((z + sign * off[0]) % z_count) * y_count + (y + sign * off[1]) % y_count

    steps = len(CORE_PLANS[0])
    table = np.zeros((steps, 3, kinds, row_count), np.int32)
    all_pairs = []
    holders = [({0}, {row_count - 1}) for _ in CORE_PLANS]
    for step in range(steps):
        new_holders = [(set(t), set(b)) for t, b in holders]
        step_pairs = []
        for slot in range(len(CORE_PLANS[0][step])):
            pairs = []
            for kind, plan in enumerate(CORE_PLANS):
                off = plan[step][slot]
                tops, bottoms = holders[kind]
                for s in tops:
                    table[step, 2, kind, s] = 1
                    d = moved(s, off, 1)
                    table[step, 0, kind, d] = slot + 1
                    new_holders[kind][0].add(d)
                for s in bottoms:
                    d = moved(s, off, -1)
                    table[step, 1, kind, d] = slot + 1
                    new_holders[kind][1].add(d)
                for c in range(kind, chain_count, kinds):
                    pairs += [(c * row_count + s, c * row_count + moved(s, off, 1)) for s in tops]
                    pairs += [(c * row_count + s, c * row_count + moved(s, off, -1)) for s in bottoms]
            step_pairs.append(pairs)
        all_pairs.append(step_pairs)
        holders = new_holders
    mine = jnp.asarray(table.reshape(steps * 3, kinds, row_count))[:, chain_pos % kinds, row_pos]
    for step in range(steps):
        sent = jnp.where(mine[3 * step + 2] == 1, top, bottom)
        got = [lax.ppermute(sent, ("chain", "rows"), pairs) for pairs in all_pairs[step]]
        top = lax.select_n(mine[3 * step], top, *got)
        bottom = lax.select_n(mine[3 * step + 1], bottom, *got)
    return top, bottom


def on_device(right_spike, left_spike, loads, tip_inverse):
    precise = lax.Precision.HIGHEST
    band = HALF_BAND
    width = LOAD_COLS
    chain_pos = lax.axis_index("chain")
    row_pos = lax.axis_index("rows")
    chain_count = lax.axis_size("chain")
    row_count = lax.axis_size("rows")
    spike_right = right_spike
    spike_left = left_spike
    load_block = loads
    inverses = [tip_inverse[0, 0]]
    for level in range(1, LEVELS):
        half = 2**level
        place = chain_pos % (2 * half)
        lasts = list(range(half - 1, chain_count - 1, 2 * half))
        mine = tip_inverse[0, level]
        for k in range(1, half):
            pairs = [(a, a - k) for a in lasts] + [(a + 1, a + 1 + k) for a in lasts]
            got = lax.ppermute(mine, "chain", pairs)
            mine = jnp.where((place == half - 1 - k) | (place == half + k), got, mine)
        inverses.append(mine)
    first_tip = jnp.concatenate([load_block[:band], spike_right[:band]], 1)
    last_tip = jnp.concatenate([load_block[-band:], spike_left[-band:]], 1)
    if row_count == 32 and chain_count % 2 == 0:
        top, bottom = core_tree(first_tip, last_tip, chain_pos, row_pos, chain_count, 8, 4)
    else:
        top, bottom = spread_tips(first_tip, last_tip, row_pos, row_count, row_fanouts(row_count))
    inverses, top, bottom = lax.optimization_barrier((inverses, top, bottom))
    blank_block = jnp.zeros((band, band), jnp.float32)
    for level in range(LEVELS):
        half = 2**level
        place = chain_pos % (2 * half)
        side_low = place < half
        lasts = list(range(half - 1, chain_count - 1, 2 * half))
        lower_tip = bottom
        upper_tip = top
        sent = jnp.where(place == half - 1, bottom, top)
        for offset in list(range(-(half - 1), 0)) + list(range(1, half + 1)):
            pairs = [(a, a + offset) for a in lasts] + [(a + 1, a + 1 - offset) for a in lasts]
            got = lax.ppermute(sent, "chain", pairs)
            lower_tip = jnp.where(place == half - 1 + offset, got, lower_tip)
            upper_tip = jnp.where(place == half - offset, got, upper_tip)
        if level > 0:
            lower_tip, upper_tip, spike_right, spike_left, load_block = lax.optimization_barrier(
                (lower_tip, upper_tip, spike_right, spike_left, load_block)
            )
        upper_rows = jnp.concatenate([lower_tip[:, :band], lower_tip[:, band:], blank_block], 1)
        lower_rows = jnp.concatenate([upper_tip[:, :band], blank_block, upper_tip[:, band:]], 1)
        tip_rhs = jnp.concatenate([upper_rows, lower_rows], 0)
        solved = jnp.dot(inverses[level], tip_rhs, precision=precise, preferred_element_type=jnp.float32)
        if level + 1 < LEVELS:
            bottom_prod = jnp.dot(
                bottom[:, band:], solved[:, : 2 * band], precision=precise, preferred_element_type=jnp.float32
            )
            bottom = jnp.concatenate([bottom[:, :band] - bottom_prod[:, :band], -bottom_prod[:, band:]], 1)
            top_prod = jnp.dot(
                top[:, band:],
                jnp.concatenate([solved[:, :band], solved[:, 2 * band :]], 1),
                precision=precise,
                preferred_element_type=jnp.float32,
            )
            top = jnp.concatenate([top[:, :band] - top_prod[:, :band], -top_prod[:, band:]], 1)
        flag = jnp.where(side_low, 1, 0).astype(jnp.int32).reshape(1)
        spike_right, spike_left, load_block = bulk_update(flag, solved, spike_right, spike_left, load_block)
    return (spike_right, spike_left, load_block)


def solution(mesh):
    in_specs = (
        P(("chain", "rows"), None),
        P(("chain", "rows"), None),
        P(("chain", "rows"), None),
        P("chain", None, None, None),
    )
    out_specs = (P(("chain", "rows"), None), P(("chain", "rows"), None), P(("chain", "rows"), None))
    return jax.shard_map(
        on_device, mesh=mesh, in_specs=in_specs, out_specs=out_specs, check_vma=False
    )
```

profile of v0, /device:TPU:31, one launch (start us, length us, event | category | flops | bytes accessed | tf_op | source)
XLA Modules:
  0.0 131.5 jit_solution(1621023796285926240)
XLA Ops:
  0.6 0.0 copy-start.8
  0.6 2.4 %slice_bitcast_fusion = (f32[256,512]{1,0:T(8,128)}, f32[256,512]{1,0:T(8,128)}, f32[256,512]{1,0:T(8,128)S(1)}) fusion(f32[1,3,256,512]{3,2,1,0:T(8,128)} %param.8), kind=kLoop, calls=%fused_computation.57 | loop fusion | bytes 3145728 | tf_op jit(solution)/shard_map/squeeze | solution.py:145
  3.1 1.5 %collective-permute-start.1 = (f32[256,512]{1,0:T(8,128)}, f32[256,512]{1,0:T(8,128)}, u32[]{:S(2)}, u32[]{:S(2)}) collective-permute-start(f32[256,512]{1,0:T(8,128)} %get-tuple-element.59), channel_id=1, source_target_pairs={{96,64},{128,160},{97,65},{129,161},{98,66},{130,162},{99,67},{131... | collective-permute-start | bytes 1572872 | tf_op jit(solution)/shard_map/ppermute | solution.py:148
  4.5 1.3 collective-permute-start
  5.9 1.0 slice.148
  6.8 0.0 copy-start
  6.8 1.1 slice.145
  7.9 0.7 fusion.64
  9.3 1.1 fusion.58
  10.4 0.9 fusion.44
  11.2 1.5 %collective-permute-start.5 = (f32[256,512]{1,0:T(8,128)}, f32[256,512]{1,0:T(8,128)}, u32[]{:S(2)}, u32[]{:S(2)}) collective-permute-start(f32[256,512]{1,0:T(8,128)} %fusion.44), channel_id=1, source_target_pairs={{0,16},{31,15},{64,80},{95,79},{128,144},{159,143},{192,208},{223,... | collective-permute-start | bytes 1572872 | tf_op jit(solution)/shard_map/ppermute | solution.py:123
  12.7 1.3 collective-permute-start.6
  14.0 1.5 %collective-permute-start.4 = (f32[256,512]{1,0:T(8,128)}, f32[256,512]{1,0:T(8,128)}, u32[]{:S(2)}, u32[]{:S(2)}) collective-permute-start(f32[256,512]{1,0:T(8,128)} %fusion.44), channel_id=1, source_target_pairs={{0,8},{31,23},{64,72},{95,87},{128,136},{159,151},{192,200},{223,2... | collective-permute-start | bytes 1572872 | tf_op jit(solution)/shard_map/ppermute | solution.py:123
  19.9 2.1 %broadcast_select_fusion.7 = (f32[256,512]{1,0:T(8,128)S(1)}, f32[256,512]{1,0:T(8,128)}) fusion(f32[256,512]{1,0:T(8,128)} %collective-permute-done.1, pred[]{:T(512)S(6)} %or.15, f32[1,3,256,512]{3,2,1,0:T(8,128)S(1)} %copy-done, f32[256,512]{1,0:T(8,128)} %collective-permute-done, pred[]{:T(512)S(6)} %or.12), kind=kLoop, calls=%fused_computation.80 | loop fusion | flops 262144 | bytes 3145730 | tf_op jit(solution)/shard_map/jit(_where)/select_n | solution.py:149
  22.0 1.5 %collective-permute-start.2 = (f32[256,512]{1,0:T(8,128)S(1)}, f32[256,512]{1,0:T(8,128)}, u32[]{:S(2)}, u32[]{:S(2)}) collective-permute-start(f32[256,512]{1,0:T(8,128)S(1)} %get-tuple-element.57), channel_id=1, source_target_pairs={{96,32},{128,192},{97,33},{129,193},{98,34},{130,194},{99,35},{131... | collective-permute-start | bytes 1572872 | tf_op jit(solution)/shard_map/ppermute | solution.py:148
  23.4 1.5 %collective-permute-done.6 = f32[256,512]{1,0:T(8,128)} collective-permute-done((f32[256,512]{1,0:T(8,128)}, f32[256,512]{1,0:T(8,128)}, u32[]{:S(2)}, u32[]{:S(2)}) %collective-permute-start.6) | collective-permute-done | bytes 524320 | tf_op jit(solution)/shard_map/ppermute | solution.py:123
  24.9 1.6 %broadcast_select_fusion.5 = (f32[256,512]{1,0:T(8,128)S(1)}, f32[256,512]{1,0:T(8,128)S(1)}, f32[256,512]{1,0:T(8,128)S(1)}) fusion(pred[]{:T(512)} %bitcast.11, f32[256,512]{1,0:T(8,128)} %collective-permute-done.5, f32[256,512]{1,0:T(8,128)} %collective-permute-done.6, pred[]{:T(512)} %bitcast.14, f32[256,512]{1,0:T(8,128)} %collective-permute-done.4, ...), kind=kLoop, calls=%fused_computation.78 | loop fusion | flops 1179648 | bytes 4194311 | tf_op jit(solution)/shard_map/jit(_where)/select_n | solution.py:122
  26.6 7.5 %collective-permute-start.8 = (f32[256,512]{1,0:T(8,128)S(1)}, f32[256,512]{1,0:T(8,128)S(1)}, u32[]{:S(2)}, u32[]{:S(2)}) collective-permute-start(f32[256,512]{1,0:T(8,128)S(1)} %get-tuple-element.48), channel_id=1, source_target_pairs={{0,2},{8,10},{16,18},{24,26},{7,5},{23,21},{15,13},{31,29},{64,66}... | collective-permute-start | bytes 1572872 | tf_op jit(solution)/shard_map/ppermute | solution.py:123
  34.1 2.1 %collective-permute-start.9 = (f32[256,512]{1,0:T(8,128)S(1)}, f32[256,512]{1,0:T(8,128)}, u32[]{:S(2)}, u32[]{:S(2)}) collective-permute-start(f32[256,512]{1,0:T(8,128)S(1)} %get-tuple-element.48), channel_id=1, source_target_pairs={{0,3},{8,11},{16,19},{24,27},{7,4},{23,20},{15,12},{31,28},{64,67}... | collective-permute-start | bytes 1572872 | tf_op jit(solution)/shard_map/ppermute | solution.py:123
  36.2 2.1 %collective-permute-start.7 = (f32[256,512]{1,0:T(8,128)S(1)}, f32[256,512]{1,0:T(8,128)}, u32[]{:S(2)}, u32[]{:S(2)}) collective-permute-start(f32[256,512]{1,0:T(8,128)S(1)} %get-tuple-element.48), channel_id=1, source_target_pairs={{0,1},{8,9},{16,17},{24,25},{7,6},{23,22},{15,14},{31,30},{64,65},... | collective-permute-start | bytes 1572872 | tf_op jit(solution)/shard_map/ppermute | solution.py:123
  42.6 0.1 broadcast_select_fusion.8
  42.7 1.3 collective-permute-start.3
  44.0 1.8 %collective-permute-done.8 = f32[256,512]{1,0:T(8,128)S(1)} collective-permute-done((f32[256,512]{1,0:T(8,128)S(1)}, f32[256,512]{1,0:T(8,128)S(1)}, u32[]{:S(2)}, u32[]{:S(2)}) %collective-permute-start.8) | collective-permute-done | bytes 524320 | tf_op jit(solution)/shard_map/ppermute | solution.py:123
  45.8 5.6 %collective-permute-done.7 = f32[256,512]{1,0:T(8,128)} collective-permute-done((f32[256,512]{1,0:T(8,128)S(1)}, f32[256,512]{1,0:T(8,128)}, u32[]{:S(2)}, u32[]{:S(2)}) %collective-permute-start.7) | collective-permute-done | bytes 524320 | tf_op jit(solution)/shard_map/ppermute | solution.py:123
  51.4 2.3 %broadcast_select_fusion.4 = (f32[256,512]{1,0:T(8,128)}, f32[256,512]{1,0:T(8,128)S(1)}, f32[256,512]{1,0:T(8,128)S(1)}) fusion(pred[]{:T(512)} %bitcast.16, f32[256,512]{1,0:T(8,128)S(1)} %collective-permute-done.8, f32[256,512]{1,0:T(8,128)} %collective-permute-done.9, pred[]{:T(512)} %bitcast.19, f32[256,512]{1,0:T(8,128)S(1)} %get-tuple-element.49, ...), kind=kLoop, calls=%fused_computation.77 | loop fusion | flops 917504 | bytes 4194311 | tf_op jit(solution)/shard_map/jit(_where)/select_n | solution.py:122
  53.7 1.5 %collective-permute-start.10 = (f32[256,512]{1,0:T(8,128)}, f32[256,512]{1,0:T(8,128)S(1)}, u32[]{:S(2)}, u32[]{:S(2)}) collective-permute-start(f32[256,512]{1,0:T(8,128)} %get-tuple-element.45), channel_id=1, source_target_pairs={{0,4},{1,5},{2,6},{3,7},{8,12},{9,13},{10,14},{11,15},{16,20},{17,... | collective-permute-start | bytes 1572872 | tf_op jit(solution)/shard_map/ppermute | solution.py:123
  56.4 2.0 %broadcast_select_fusion.9 = f32[256,512]{1,0:T(8,128)} fusion(f32[256,512]{1,0:T(8,128)} %collective-permute-done.3, f32[256,512]{1,0:T(8,128)S(1)} %broadcast_select_fusion.8, pred[]{:T(512)S(6)} %or.13), kind=kLoop, calls=%fused_computation.82 | loop fusion | flops 131072 | bytes 1572865 | tf_op jit(solution)/shard_map/jit(_where)/select_n | solution.py:149
  58.4 4.7 %collective-permute-done.10 = f32[256,512]{1,0:T(8,128)S(1)} collective-permute-done((f32[256,512]{1,0:T(8,128)}, f32[256,512]{1,0:T(8,128)S(1)}, u32[]{:S(2)}, u32[]{:S(2)}) %collective-permute-start.10) | collective-permute-done | bytes 524320 | tf_op jit(solution)/shard_map/ppermute | solution.py:123
  63.2 0.1 broadcast_select_fusion.3
  63.3 0.1 broadcast_select_fusion.1
  63.4 0.1 collective-permute-start.11
  63.5 0.0 copy-start.4
  63.5 1.9 %collective-permute-done.11 = f32[256,512]{1,0:T(8,128)S(1)} collective-permute-done((f32[256,512]{1,0:T(8,128)S(1)}, f32[256,512]{1,0:T(8,128)S(1)}, u32[]{:S(2)}, u32[]{:S(2)}) %collective-permute-start.11) | collective-permute-done | bytes 524320 | tf_op jit(solution)/shard_map/ppermute | solution.py:169
  65.4 0.1 broadcast_select_fusion
  65.6 1.5 %fusion.2.x_ref = f32[256,768]{1,0:T(8,128)S(1)} fusion(f32[256,512]{1,0:T(8,128)S(1)} %copy-done.4, f32[256,256]{1,0:T(8,128)S(1)} %broadcast_in_dim.3, f32[256,512]{1,0:T(8,128)S(1)} %get-tuple-element.81, f32[256,256]{1,0:T(8,128)S(1)} %get-tuple-element.79, f32[256,256]{1,0:T(8,128)S(1)} %get-tuple-element.78), kind=kOutput, calls=%fused_computation.5 | convolution fusion | flops 1209925632 | bytes 2621440 | tf_op jit(solution)/shard_map/dot_general | solution.py:179
  67.2 0.6 fusion.32
  67.8 0.6 fusion.34
  68.4 0.1 slice_subtract_fusion.2
  68.6 0.1 fusion.43
  68.6 1.3 collective-permute-start.12
  69.9 1.5 %collective-permute-start.13 = (f32[256,512]{1,0:T(8,128)S(1)}, f32[256,512]{1,0:T(8,128)}, u32[]{:S(2)}, u32[]{:S(2)}) collective-permute-start(f32[256,512]{1,0:T(8,128)S(1)} %fusion.43), channel_id=1, source_target_pairs={{32,64},{160,192},{64,32},{192,160},{33,65},{161,193},{65,33},{193... | collective-permute-start | bytes 1572872 | tf_op jit(solution)/shard_map/ppermute | solution.py:169
  71.4 1.3 collective-permute-start.14
  72.7 6.9 %shard_map.76 = (f32[2048,256]{1,0:T(8,128)}, f32[2048,256]{1,0:T(8,128)}, f32[2048,256]{1,0:T(8,128)}) custom-call(s32[1]{0:T(128)} %bitcast.21.flag_ref, f32[256,768]{1,0:T(8,128)} %copy-done.2, f32[2048,256]{1,0:T(8,128)} %v_ref.1, f32[2048,256]{1,0:T(8,128)} %w_ref.1, f32[2048,256]{1,0:T(8,128)} %g_ref.1), custom_call_target="tpu_custom_call" | custom-call | tf_op jit(solution)/shard_map/pallas_call | solution.py:67
  79.7 3.4 %collective-permute-done.12 = f32[256,512]{1,0:T(8,128)S(1)} collective-permute-done((f32[256,512]{1,0:T(8,128)S(1)}, f32[256,512]{1,0:T(8,128)S(1)}, u32[]{:S(2)}, u32[]{:S(2)}) %collective-permute-start.12) | collective-permute-done | bytes 524320 | tf_op jit(solution)/shard_map/ppermute | solution.py:169
  83.1 1.4 %select_select_fusion.2 = (f32[256,512]{1,0:T(8,128)S(1)}, f32[256,512]{1,0:T(8,128)S(1)}) fusion(f32[256,512]{1,0:T(8,128)S(1)} %collective-permute-done.12, f32[256,512]{1,0:T(8,128)} %collective-permute-done.13, f32[256,512]{1,0:T(8,128)} %collective-permute-done.14, f32[256,256]{1,0:T(8,128)S(1)} %get-tuple-element.77, ...), kind=kLoop, calls=%fused_computation.51 | loop fusion | flops 1048576 | bytes 3670020 | tf_op jit(solution)/shard_map/jit(_where)/select_n | solution.py:171
  84.6 1.5 %fusion.6.x_ref = f32[256,768]{1,0:T(8,128)S(1)} fusion(f32[256,512]{1,0:T(8,128)S(1)} %copy-done.5, f32[256,256]{1,0:T(8,128)S(1)} %broadcast_in_dim.3, f32[256,512]{1,0:T(8,128)S(1)} %get-tuple-element.32, f32[256,256]{1,0:T(8,128)S(1)} %get-tuple-element.73, f32[256,256]{1,0:T(8,128)S(1)} %get-tuple-element.72), kind=kOutput, calls=%fused_computation.8 | convolution fusion | flops 1209925632 | bytes 2621440 | tf_op jit(solution)/shard_map/dot_general | solution.py:179
  86.1 0.6 fusion.30
  86.8 0.6 fusion.38
  87.4 0.1 slice_subtract_fusion
  87.5 0.1 slice_subtract_fusion.1
  87.5 0.9 fusion.42
  88.4 1.5 %collective-permute-start.15 = (f32[256,512]{1,0:T(8,128)}, f32[256,512]{1,0:T(8,128)S(1)}, u32[]{:S(2)}, u32[]{:S(2)}) collective-permute-start(f32[256,512]{1,0:T(8,128)} %fusion.42), channel_id=1, source_target_pairs={{96,224},{128,0},{97,225},{129,1},{98,226},{130,2},{99,227},{131,3... | collective-permute-start | bytes 1572872 | tf_op jit(solution)/shard_map/ppermute | solution.py:169
  89.9 0.7 collective-permute-start.16
  90.6 0.7 collective-permute-start.17
  91.3 0.7 collective-permute-start.18
  92.0 1.5 %collective-permute-start.19 = (f32[256,512]{1,0:T(8,128)}, f32[256,512]{1,0:T(8,128)}, u32[]{:S(2)}, u32[]{:S(2)}) collective-permute-start(f32[256,512]{1,0:T(8,128)} %fusion.42), channel_id=1, source_target_pairs={{96,64},{128,160},{97,65},{129,161},{98,66},{130,162},{99,67},{131... | collective-permute-start | bytes 1572872 | tf_op jit(solution)/shard_map/ppermute | solution.py:169
  93.5 6.5 %collective-permute-done.15 = f32[256,512]{1,0:T(8,128)S(1)} collective-permute-done((f32[256,512]{1,0:T(8,128)}, f32[256,512]{1,0:T(8,128)S(1)}, u32[]{:S(2)}, u32[]{:S(2)}) %collective-permute-start.15) | collective-permute-done | bytes 524320 | tf_op jit(solution)/shard_map/ppermute | solution.py:169
  100.1 1.5 %collective-permute-start.20 = (f32[256,512]{1,0:T(8,128)}, f32[256,512]{1,0:T(8,128)}, u32[]{:S(2)}, u32[]{:S(2)}) collective-permute-start(f32[256,512]{1,0:T(8,128)} %fusion.42), channel_id=1, source_target_pairs={{96,32},{128,192},{97,33},{129,193},{98,34},{130,194},{99,35},{131... | collective-permute-start | bytes 1572872 | tf_op jit(solution)/shard_map/ppermute | solution.py:169
  101.5 1.3 collective-permute-start.21
  102.8 6.9 %shard_map.77 = (f32[2048,256]{1,0:T(8,128)}, f32[2048,256]{1,0:T(8,128)}, f32[2048,256]{1,0:T(8,128)}) custom-call(s32[1]{0:T(128)} %bitcast.22.flag_ref, f32[256,768]{1,0:T(8,128)} %copy-done.1, f32[2048,256]{1,0:T(8,128)} %get-tuple-element.34.v_ref, f32[2048,256]{1,0:T(8,128)} %get-tuple-element.35.w_ref, f32[2048,256]{1,0:T(8,128)} %get-tuple-element.36.g_ref), custom_call_target="tpu_custom_call" | custom-call | tf_op jit(solution)/shard_map/pallas_call | solution.py:67
  109.8 10.5 %collective-permute-done.21 = f32[256,512]{1,0:T(8,128)} collective-permute-done((f32[256,512]{1,0:T(8,128)}, f32[256,512]{1,0:T(8,128)}, u32[]{:S(2)}, u32[]{:S(2)}) %collective-permute-start.21) | collective-permute-done | bytes 524320 | tf_op jit(solution)/shard_map/ppermute | solution.py:169
  120.3 1.9 %select_select_fusion = (f32[256,512]{1,0:T(8,128)S(1)}, f32[256,512]{1,0:T(8,128)S(1)}) fusion(f32[256,512]{1,0:T(8,128)S(1)} %collective-permute-done.15, f32[256,512]{1,0:T(8,128)S(1)} %collective-permute-done.16, f32[256,512]{1,0:T(8,128)S(1)} %collective-permute-done.17, f32[256,512]{1,0:T(8,128)S(1)} %collective-permute-done.18, ...), kind=kLoop, calls=%fused_computation.49 | loop fusion | flops 2097152 | bytes 5767176 | tf_op jit(solution)/shard_map/jit(_where)/select_n | solution.py:171
  122.2 2.4 %fusion.10.x_ref = f32[256,768]{1,0:T(8,128)} fusion(f32[256,512]{1,0:T(8,128)S(1)} %copy-done.3, f32[256,256]{1,0:T(8,128)S(1)} %copy-done.7, f32[256,512]{1,0:T(8,128)S(1)} %get-tuple-element.40, f32[256,256]{1,0:T(8,128)S(1)} %get-tuple-element.67, f32[256,256]{1,0:T(8,128)S(1)} %get-tuple-element.66), kind=kOutput, calls=%fused_computation.11 | convolution fusion | flops 1209925632 | bytes 2621440 | tf_op jit(solution)/shard_map/dot_general | solution.py:179
  124.6 6.9 %shard_map.78 = (f32[2048,256]{1,0:T(8,128)}, f32[2048,256]{1,0:T(8,128)}, f32[2048,256]{1,0:T(8,128)}) custom-call(s32[1]{0:T(128)} %bitcast.flag_ref, f32[256,768]{1,0:T(8,128)} %fusion.10.x_ref, f32[2048,256]{1,0:T(8,128)} %get-tuple-element.42.v_ref, f32[2048,256]{1,0:T(8,128)} %get-tuple-element.43.w_ref, f32[2048,256]{1,0:T(8,128)} %get-tuple-element.44.g_ref), custom_call_target="tpu_custom_call" | custom-call | tf_op jit(solution)/shard_map/pallas_call | solution.py:67
  (35 shorter events, 0.3 us)
Async XLA Ops:
  0.6 7.3 %copy-start.8 = (s32[9,2,32]{2,1,0:T(2,128)S(1)}, s32[9,2,32]{2,1,0:T(2,128)}, u32[]{:S(2)}) copy-start(s32[9,2,32]{2,1,0:T(2,128)} %constant.82.clone) | copy-start | bytes 6916
  3.1 16.8 %collective-permute-start.1 = (f32[256,512]{1,0:T(8,128)}, f32[256,512]{1,0:T(8,128)}, u32[]{:S(2)}, u32[]{:S(2)}) collective-permute-start(f32[256,512]{1,0:T(8,128)} %get-tuple-element.59), channel_id=1, source_target_pairs={{96,64},{128,160},{97,65},{129,161},{98,66},{130,162},{99,67},{131... | collective-permute-start | bytes 1572872 | tf_op jit(solution)/shard_map/ppermute | solution.py:148
  4.5 15.3 %collective-permute-start = (f32[256,512]{1,0:T(8,128)S(1)}, f32[256,512]{1,0:T(8,128)}, u32[]{:S(2)}, u32[]{:S(2)}) collective-permute-start(f32[256,512]{1,0:T(8,128)S(1)} %get-tuple-element.61), channel_id=1, source_target_pairs={{32,0},{160,128},{64,96},{192,224},{33,1},{161,129},{65,97},{193,2... | collective-permute-start | bytes 1572872 | tf_op jit(solution)/shard_map/ppermute | solution.py:148
  6.8 13.1 %copy-start = (f32[1,3,256,512]{3,2,1,0:T(8,128)S(1)}, f32[1,3,256,512]{3,2,1,0:T(8,128)}, u32[]{:S(2)}) copy-start(f32[1,3,256,512]{3,2,1,0:T(8,128)} %param.8) | copy-start | bytes 4718596
  11.2 12.2 %collective-permute-start.5 = (f32[256,512]{1,0:T(8,128)}, f32[256,512]{1,0:T(8,128)}, u32[]{:S(2)}, u32[]{:S(2)}) collective-permute-start(f32[256,512]{1,0:T(8,128)} %fusion.44), channel_id=1, source_target_pairs={{0,16},{31,15},{64,80},{95,79},{128,144},{159,143},{192,208},{223,... | collective-permute-start | bytes 1572872 | tf_op jit(solution)/shard_map/ppermute | solution.py:123
  12.7 12.3 %collective-permute-start.6 = (f32[256,512]{1,0:T(8,128)}, f32[256,512]{1,0:T(8,128)}, u32[]{:S(2)}, u32[]{:S(2)}) collective-permute-start(f32[256,512]{1,0:T(8,128)} %fusion.44), channel_id=1, source_target_pairs={{0,24},{31,7},{64,88},{95,71},{128,152},{159,135},{192,216},{223,1... | collective-permute-start | bytes 1572872 | tf_op jit(solution)/shard_map/ppermute | solution.py:123
  14.0 11.0 %collective-permute-start.4 = (f32[256,512]{1,0:T(8,128)}, f32[256,512]{1,0:T(8,128)}, u32[]{:S(2)}, u32[]{:S(2)}) collective-permute-start(f32[256,512]{1,0:T(8,128)} %fusion.44), channel_id=1, source_target_pairs={{0,8},{31,23},{64,72},{95,87},{128,136},{159,151},{192,200},{223,2... | collective-permute-start | bytes 1572872 | tf_op jit(solution)/shard_map/ppermute | solution.py:123
  22.0 20.6 %collective-permute-start.2 = (f32[256,512]{1,0:T(8,128)S(1)}, f32[256,512]{1,0:T(8,128)}, u32[]{:S(2)}, u32[]{:S(2)}) collective-permute-start(f32[256,512]{1,0:T(8,128)S(1)} %get-tuple-element.57), channel_id=1, source_target_pairs={{96,32},{128,192},{97,33},{129,193},{98,34},{130,194},{99,35},{131... | collective-permute-start | bytes 1572872 | tf_op jit(solution)/shard_map/ppermute | solution.py:148
  26.6 19.2 %collective-permute-start.8 = (f32[256,512]{1,0:T(8,128)S(1)}, f32[256,512]{1,0:T(8,128)S(1)}, u32[]{:S(2)}, u32[]{:S(2)}) collective-permute-start(f32[256,512]{1,0:T(8,128)S(1)} %get-tuple-element.48), channel_id=1, source_target_pairs={{0,2},{8,10},{16,18},{24,26},{7,5},{23,21},{15,13},{31,29},{64,66}... | collective-permute-start | bytes 1572872 | tf_op jit(solution)/shard_map/ppermute | solution.py:123
  34.1 11.7 %collective-permute-start.9 = (f32[256,512]{1,0:T(8,128)S(1)}, f32[256,512]{1,0:T(8,128)}, u32[]{:S(2)}, u32[]{:S(2)}) collective-permute-start(f32[256,512]{1,0:T(8,128)S(1)} %get-tuple-element.48), channel_id=1, source_target_pairs={{0,3},{8,11},{16,19},{24,27},{7,4},{23,20},{15,12},{31,28},{64,67}... | collective-permute-start | bytes 1572872 | tf_op jit(solution)/shard_map/ppermute | solution.py:123
  36.2 15.2 %collective-permute-start.7 = (f32[256,512]{1,0:T(8,128)S(1)}, f32[256,512]{1,0:T(8,128)}, u32[]{:S(2)}, u32[]{:S(2)}) collective-permute-start(f32[256,512]{1,0:T(8,128)S(1)} %get-tuple-element.48), channel_id=1, source_target_pairs={{0,1},{8,9},{16,17},{24,25},{7,6},{23,22},{15,14},{31,30},{64,65},... | collective-permute-start | bytes 1572872 | tf_op jit(solution)/shard_map/ppermute | solution.py:123
  42.7 13.8 %collective-permute-start.3 = (f32[256,512]{1,0:T(8,128)S(1)}, f32[256,512]{1,0:T(8,128)}, u32[]{:S(2)}, u32[]{:S(2)}) collective-permute-start(f32[256,512]{1,0:T(8,128)S(1)} %broadcast_select_fusion.8), channel_id=1, source_target_pairs={{96,0},{128,224},{97,1},{129,225},{98,2},{130,226},{99,3},{131,227... | collective-permute-start | bytes 1572872 | tf_op jit(solution)/shard_map/ppermute | solution.py:148
  53.7 9.5 %collective-permute-start.10 = (f32[256,512]{1,0:T(8,128)}, f32[256,512]{1,0:T(8,128)S(1)}, u32[]{:S(2)}, u32[]{:S(2)}) collective-permute-start(f32[256,512]{1,0:T(8,128)} %get-tuple-element.45), channel_id=1, source_target_pairs={{0,4},{1,5},{2,6},{3,7},{8,12},{9,13},{10,14},{11,15},{16,20},{17,... | collective-permute-start | bytes 1572872 | tf_op jit(solution)/shard_map/ppermute | solution.py:123
  63.4 2.0 %collective-permute-start.11 = (f32[256,512]{1,0:T(8,128)S(1)}, f32[256,512]{1,0:T(8,128)S(1)}, u32[]{:S(2)}, u32[]{:S(2)}) collective-permute-start(f32[256,512]{1,0:T(8,128)S(1)} %broadcast_select_fusion.1), channel_id=1, source_target_pairs={{0,32},{64,96},{128,160},{192,224},{32,0},{96,64},{160,128},{224,1... | collective-permute-start | bytes 1572872 | tf_op jit(solution)/shard_map/ppermute | solution.py:169
  63.5 2.1 %copy-start.4 = (f32[256,512]{1,0:T(8,128)S(1)}, f32[256,512]{1,0:T(8,128)}, u32[]{:S(2)}) copy-start(f32[256,512]{1,0:T(8,128)} %get-tuple-element.26) | copy-start | bytes 1572868
  65.6 18.9 %copy-start.6 = (f32[256,256]{1,0:T(8,128)}, f32[256,256]{1,0:T(8,128)S(1)}, u32[]{:S(2)}) copy-start(f32[256,256]{1,0:T(8,128)S(1)} %broadcast_in_dim.3) | copy-start | bytes 786436
  67.1 1.3 copy-start.2
  68.6 14.4 %collective-permute-start.12 = (f32[256,512]{1,0:T(8,128)S(1)}, f32[256,512]{1,0:T(8,128)S(1)}, u32[]{:S(2)}, u32[]{:S(2)}) collective-permute-start(f32[256,512]{1,0:T(8,128)S(1)} %fusion.43), channel_id=1, source_target_pairs={{32,96},{160,224},{64,0},{192,128},{33,97},{161,225},{65,1},{193,1... | collective-permute-start | bytes 1572872 | tf_op jit(solution)/shard_map/ppermute | solution.py:169
  69.9 13.1 %collective-permute-start.13 = (f32[256,512]{1,0:T(8,128)S(1)}, f32[256,512]{1,0:T(8,128)}, u32[]{:S(2)}, u32[]{:S(2)}) collective-permute-start(f32[256,512]{1,0:T(8,128)S(1)} %fusion.43), channel_id=1, source_target_pairs={{32,64},{160,192},{64,32},{192,160},{33,65},{161,193},{65,33},{193... | collective-permute-start | bytes 1572872 | tf_op jit(solution)/shard_map/ppermute | solution.py:169
  71.4 11.7 %collective-permute-start.14 = (f32[256,512]{1,0:T(8,128)S(1)}, f32[256,512]{1,0:T(8,128)}, u32[]{:S(2)}, u32[]{:S(2)}) collective-permute-start(f32[256,512]{1,0:T(8,128)S(1)} %fusion.43), channel_id=1, source_target_pairs={{32,0},{160,128},{64,96},{192,224},{33,1},{161,129},{65,97},{193,2... | collective-permute-start | bytes 1572872 | tf_op jit(solution)/shard_map/ppermute | solution.py:169
  79.7 4.9 %copy-start.5 = (f32[256,512]{1,0:T(8,128)S(1)}, f32[256,512]{1,0:T(8,128)}, u32[]{:S(2)}) copy-start(f32[256,512]{1,0:T(8,128)} %get-tuple-element.28) | copy-start | bytes 1572868
  86.1 1.3 copy-start.1
  88.4 11.6 %collective-permute-start.15 = (f32[256,512]{1,0:T(8,128)}, f32[256,512]{1,0:T(8,128)S(1)}, u32[]{:S(2)}, u32[]{:S(2)}) collective-permute-start(f32[256,512]{1,0:T(8,128)} %fusion.42), channel_id=1, source_target_pairs={{96,224},{128,0},{97,225},{129,1},{98,226},{130,2},{99,227},{131,3... | collective-permute-start | bytes 1572872 | tf_op jit(solution)/shard_map/ppermute | solution.py:169
  89.9 11.6 %collective-permute-start.16 = (f32[256,512]{1,0:T(8,128)}, f32[256,512]{1,0:T(8,128)S(1)}, u32[]{:S(2)}, u32[]{:S(2)}) collective-permute-start(f32[256,512]{1,0:T(8,128)} %fusion.42), channel_id=1, source_target_pairs={{96,192},{128,32},{97,193},{129,33},{98,194},{130,34},{99,195},{13... | collective-permute-start | bytes 1572872 | tf_op jit(solution)/shard_map/ppermute | solution.py:169
  90.6 19.2 %collective-permute-start.17 = (f32[256,512]{1,0:T(8,128)}, f32[256,512]{1,0:T(8,128)S(1)}, u32[]{:S(2)}, u32[]{:S(2)}) collective-permute-start(f32[256,512]{1,0:T(8,128)} %fusion.42), channel_id=1, source_target_pairs={{96,160},{128,64},{97,161},{129,65},{98,162},{130,66},{99,163},{13... | collective-permute-start | bytes 1572872 | tf_op jit(solution)/shard_map/ppermute | solution.py:169
  91.3 18.5 %collective-permute-start.18 = (f32[256,512]{1,0:T(8,128)}, f32[256,512]{1,0:T(8,128)S(1)}, u32[]{:S(2)}, u32[]{:S(2)}) collective-permute-start(f32[256,512]{1,0:T(8,128)} %fusion.42), channel_id=1, source_target_pairs={{96,128},{128,96},{97,129},{129,97},{98,130},{130,98},{99,131},{13... | collective-permute-start | bytes 1572872 | tf_op jit(solution)/shard_map/ppermute | solution.py:169
  92.0 17.8 %collective-permute-start.19 = (f32[256,512]{1,0:T(8,128)}, f32[256,512]{1,0:T(8,128)}, u32[]{:S(2)}, u32[]{:S(2)}) collective-permute-start(f32[256,512]{1,0:T(8,128)} %fusion.42), channel_id=1, source_target_pairs={{96,64},{128,160},{97,65},{129,161},{98,66},{130,162},{99,67},{131... | collective-permute-start | bytes 1572872 | tf_op jit(solution)/shard_map/ppermute | solution.py:169
  100.1 9.8 %collective-permute-start.20 = (f32[256,512]{1,0:T(8,128)}, f32[256,512]{1,0:T(8,128)}, u32[]{:S(2)}, u32[]{:S(2)}) collective-permute-start(f32[256,512]{1,0:T(8,128)} %fusion.42), channel_id=1, source_target_pairs={{96,32},{128,192},{97,33},{129,193},{98,34},{130,194},{99,35},{131... | collective-permute-start | bytes 1572872 | tf_op jit(solution)/shard_map/ppermute | solution.py:169
  101.5 18.8 %collective-permute-start.21 = (f32[256,512]{1,0:T(8,128)}, f32[256,512]{1,0:T(8,128)}, u32[]{:S(2)}, u32[]{:S(2)}) collective-permute-start(f32[256,512]{1,0:T(8,128)} %fusion.42), channel_id=1, source_target_pairs={{96,0},{128,224},{97,1},{129,225},{98,2},{130,226},{99,3},{131,227... | collective-permute-start | bytes 1572872 | tf_op jit(solution)/shard_map/ppermute | solution.py:169
  109.8 12.4 %copy-start.3 = (f32[256,512]{1,0:T(8,128)S(1)}, f32[256,512]{1,0:T(8,128)}, u32[]{:S(2)}) copy-start(f32[256,512]{1,0:T(8,128)} %broadcast_select_fusion.9) | copy-start | bytes 1572868
  109.8 12.4 %copy-start.7 = (f32[256,256]{1,0:T(8,128)S(1)}, f32[256,256]{1,0:T(8,128)}, u32[]{:S(2)}) copy-start(f32[256,256]{1,0:T(8,128)} %copy-done.6) | copy-start | bytes 786436
where the time goes:
time: 132 us
  waiting for transfers between devices  36 us (27%)
  starting transfers between devices  34.8 us (26%)
  Pallas kernels  20.8 us (16%)
  other arithmetic  13.8 us (10%)
  between operations  11.8 us (9%)
  matrix products  7.78 us (6%)
  local copies, waits for them, and re-layouts  6.51 us (5%)
    ppermute x11, waiting for transfers between devices, on_device(): got = lax.ppermute(sent, 'chain', pairs)  22.3 us
    pallas_call x3, Pallas kernels, bulk_update(): pl.pallas_call(bulk_kernel, grid_spec=pltpu.PrefetchScalarGridSpec(num_sc...  20.8 us
    ppermute x7, starting transfers between devices, core_tree(): lax.ppermute(sent, ('chain', 'rows'), pairs)  17.4 us
    ppermute x7, waiting for transfers between devices, core_tree(): lax.ppermute(sent, ('chain', 'rows'), pairs)  13.7 us
    ppermute x11, starting transfers between devices, on_device(): got = lax.ppermute(sent, 'chain', pairs)  11.9 us
    ppermute x4, starting transfers between devices, on_device(): got = lax.ppermute(mine, 'chain', pairs)  5.49 us
    dot_general x3, matrix products, on_device(): jnp.dot(inverses[level], tip_rhs, precision=precise, preferred_element_ty...  5.32 us
    select_n x3, other arithmetic, core_tree(): sent = jnp.where(mine[3 * step + 2] == 1, top, bottom)  4.8 us
  transfers between devices with their start and end apart: 22, of which 8 were waited for; matrix products, arithmetic and copies ran while one was open for 10% of the time, Pallas kernels for 11%

commit v1 on v0

--- a/solution.py
+++ b/solution.py
@@ -82,7 +82,7 @@
 )
 
 
-def core_tree(top, bottom, chain_pos, row_pos, chain_count, z_count, y_count):
+def core_tree(top, bottom, chain_pos, row_pos, chain_count, z_count, y_count, rider):
     row_count = z_count * y_count
     kinds = len(CORE_PLANS)
 
@@ -123,7 +123,9 @@
         got = [lax.ppermute(sent, ("chain", "rows"), pairs) for pairs in all_pairs[step]]
         top = lax.select_n(mine[3 * step], top, *got)
         bottom = lax.select_n(mine[3 * step + 1], bottom, *got)
-    return top, bottom
+        if step == 0:
+            rider, top, bottom = lax.optimization_barrier((rider, top, bottom))
+    return top, bottom, rider
 
 
 def on_device(right_spike, left_spike, loads, tip_inverse):
@@ -137,6 +139,12 @@
     spike_right = right_spike
     spike_left = left_spike
     load_block = loads
+    first_tip = jnp.concatenate([load_block[:band], spike_right[:band]], 1)
+    last_tip = jnp.concatenate([load_block[-band:], spike_left[-band:]], 1)
+    if row_count == 32 and chain_count % 2 == 0:
+        top, bottom, tip_inverse = core_tree(first_tip, last_tip, chain_pos, row_pos, chain_count, 8, 4, tip_inverse)
+    else:
+        top, bottom = spread_tips(first_tip, last_tip, row_pos, row_count, row_fanouts(row_count))
     inverses = [tip_inverse[0, 0]]
     for level in range(1, LEVELS):
         half = 2**level
@@ -148,12 +156,6 @@
             got = lax.ppermute(mine, "chain", pairs)
             mine = jnp.where((place == half - 1 - k) | (place == half + k), got, mine)
         inverses.append(mine)
-    first_tip = jnp.concatenate([load_block[:band], spike_right[:band]], 1)
-    last_tip = jnp.concatenate([load_block[-band:], spike_left[-band:]], 1)
-    if row_count == 32 and chain_count % 2 == 0:
-        top, bottom = core_tree(first_tip, last_tip, chain_pos, row_pos, chain_count, 8, 4)
-    else:
-        top, bottom = spread_tips(first_tip, last_tip, row_pos, row_count, row_fanouts(row_count))
     inverses, top, bottom = lax.optimization_barrier((inverses, top, bottom))
     blank_block = jnp.zeros((band, band), jnp.float32)
     for level in range(LEVELS):

time: 132 us -> 133 us (level)
  the two profiles are of different devices: /device:TPU:31 before, /device:TPU:32 now
where the time goes in v1:
time: 133 us; the launch traced here: 132 us
  waiting for transfers between devices  44.1 us (33%)
  starting transfers between devices  26.6 us (20%)
  Pallas kernels  20.9 us (16%)
  other arithmetic  14.8 us (11%)
  between operations  12.1 us (9%)
  matrix products  7.78 us (6%)
  local copies, waits for them, and re-layouts  6.09 us (5%)
    pallas_call x3, Pallas kernels, bulk_update(): pl.pallas_call(bulk_kernel, grid_spec=pltpu.PrefetchScalarGridSpec(num_sc...  20.9 us
    ppermute x7, waiting for transfers between devices, core_tree(): lax.ppermute(sent, ('chain', 'rows'), pairs)  18.3 us
    ppermute x11, waiting for transfers between devices, on_device(): got = lax.ppermute(sent, 'chain', pairs)  18.3 us
    ppermute x11, starting transfers between devices, on_device(): got = lax.ppermute(sent, 'chain', pairs)  11.2 us
    ppermute x7, starting transfers between devices, core_tree(): lax.ppermute(sent, ('chain', 'rows'), pairs)  10.7 us
    ppermute x4, waiting for transfers between devices, on_device(): got = lax.ppermute(mine, 'chain', pairs)  7.41 us
    select_n x3, other arithmetic, on_device(): mine = jnp.where((place == half - 1 - k) | (place == half + k), got, mine)  5.32 us
    dot_general x3, matrix products, on_device(): jnp.dot(inverses[level], tip_rhs, precision=precise, preferred_element_ty...  5.31 us
  transfers between devices with their start and end apart: 22, of which 7 were waited for; matrix products, arithmetic and copies ran while one was open for 5% of the time, Pallas kernels for 11%

profile of v1, /device:TPU:32, one launch (start us, length us, event | category | flops | bytes accessed | tf_op | source)
XLA Modules:
  0.0 132.2 jit_solution(7434907227410558399)
XLA Ops:
  0.6 0.0 copy-start.14
  0.7 1.0 slice.143
  1.6 1.1 fusion.58
  2.7 1.1 slice.140
  3.8 0.7 fusion.64
  5.1 0.1 fusion.44
  5.2 0.7 collective-permute-start.1
  5.9 0.7 collective-permute-start.2
  6.6 0.7 collective-permute-start
  11.2 1.3 %select_select_fusion.6 = (f32[256,512]{1,0:T(8,128)S(1)}, f32[256,512]{1,0:T(8,128)S(1)}) fusion(f32[256,512]{1,0:T(8,128)S(1)} %collective-permute-done.1, f32[256,512]{1,0:T(8,128)S(1)} %collective-permute-done.2, f32[256,512]{1,0:T(8,128)S(1)} %collective-permute-done, f32[256,256]{1,0:T(8,128)S(1)} %slice.143, f32[256,256]{1,0:T(8,128)} %copy-done.7, ...), kind=kLoop, calls=%fused_computation.58 | loop fusion | flops 1048576 | bytes 3670022 | tf_op jit(solution)/shard_map/select_n | solution.py:125
  12.5 0.1 copy-done
  12.7 1.2 slice_bitcast_fusion
  13.8 1.5 %collective-permute-start.4 = (f32[256,512]{1,0:T(8,128)}, f32[256,512]{1,0:T(8,128)}, u32[]{:S(2)}, u32[]{:S(2)}) collective-permute-start(f32[256,512]{1,0:T(8,128)} %get-tuple-element.62), channel_id=1, source_target_pairs={{96,64},{128,160},{97,65},{129,161},{98,66},{130,162},{99,67},{131... | collective-permute-start | bytes 1572872 | tf_op jit(solution)/shard_map/ppermute | solution.py:156
  15.3 1.3 collective-permute-start.3
  17.3 0.9 broadcast_select_fusion.5
  18.1 0.7 collective-permute-start.8
  18.8 1.3 collective-permute-start.9
  20.1 1.5 %collective-permute-start.7 = (f32[256,512]{1,0:T(8,128)}, f32[256,512]{1,0:T(8,128)}, u32[]{:S(2)}, u32[]{:S(2)}) collective-permute-start(f32[256,512]{1,0:T(8,128)} %broadcast_select_fusion.5), channel_id=1, source_target_pairs={{0,1},{8,9},{16,17},{24,25},{7,6},{23,22},{15,14},{31,30},{64,65},... | collective-permute-start | bytes 1572872 | tf_op jit(solution)/shard_map/ppermute | solution.py:123
  21.6 2.2 %broadcast_select_fusion.7 = (f32[256,512]{1,0:T(8,128)}, f32[256,512]{1,0:T(8,128)}) fusion(f32[256,512]{1,0:T(8,128)} %collective-permute-done.4, pred[]{:T(512)S(6)} %or.15, f32[1,3,256,512]{3,2,1,0:T(8,128)S(1)} %copy-done, f32[256,512]{1,0:T(8,128)} %collective-permute-done.3, pred[]{:T(512)S(6)} %or.12), kind=kLoop, calls=%fused_computation.80 | loop fusion | flops 262144 | bytes 3145730 | tf_op jit(solution)/shard_map/jit(_where)/select_n | solution.py:157
  23.8 0.7 collective-permute-start.5
  28.9 13.6 %collective-permute-done.9 = f32[256,512]{1,0:T(8,128)} collective-permute-done((f32[256,512]{1,0:T(8,128)}, f32[256,512]{1,0:T(8,128)}, u32[]{:S(2)}, u32[]{:S(2)}) %collective-permute-start.9) | collective-permute-done | bytes 524320 | tf_op jit(solution)/shard_map/ppermute | solution.py:123
  42.5 1.7 %broadcast_select_fusion.4 = (f32[256,512]{1,0:T(8,128)S(1)}, f32[256,512]{1,0:T(8,128)S(1)}, f32[256,512]{1,0:T(8,128)S(1)}) fusion(pred[]{:T(512)} %bitcast.16, f32[256,512]{1,0:T(8,128)} %copy-done.8, f32[256,512]{1,0:T(8,128)} %collective-permute-done.9, pred[]{:T(512)} %bitcast.19, f32[256,512]{1,0:T(8,128)S(1)} %get-tuple-element.29, ...), kind=kLoop, calls=%fused_computation.77 | loop fusion | flops 917504 | bytes 4194311 | tf_op jit(solution)/shard_map/jit(_where)/select_n | solution.py:122
  44.2 5.2 %collective-permute-start.10 = (f32[256,512]{1,0:T(8,128)S(1)}, f32[256,512]{1,0:T(8,128)S(1)}, u32[]{:S(2)}, u32[]{:S(2)}) collective-permute-start(f32[256,512]{1,0:T(8,128)S(1)} %get-tuple-element.51), channel_id=1, source_target_pairs={{0,4},{1,5},{2,6},{3,7},{8,12},{9,13},{10,14},{11,15},{16,20},{17,... | collective-permute-start | bytes 1572872 | tf_op jit(solution)/shard_map/ppermute | solution.py:123
  49.4 1.1 broadcast_select_fusion.8
  50.5 1.3 collective-permute-start.6
  53.1 4.8 %collective-permute-done.10 = f32[256,512]{1,0:T(8,128)S(1)} collective-permute-done((f32[256,512]{1,0:T(8,128)S(1)}, f32[256,512]{1,0:T(8,128)S(1)}, u32[]{:S(2)}, u32[]{:S(2)}) %collective-permute-start.10) | collective-permute-done | bytes 524320 | tf_op jit(solution)/shard_map/ppermute | solution.py:123
  57.8 0.1 broadcast_select_fusion.3
  58.0 7.4 %collective-permute-done.6 = f32[256,512]{1,0:T(8,128)} collective-permute-done((f32[256,512]{1,0:T(8,128)S(1)}, f32[256,512]{1,0:T(8,128)}, u32[]{:S(2)}, u32[]{:S(2)}) %collective-permute-start.6) | collective-permute-done | bytes 524320 | tf_op jit(solution)/shard_map/ppermute | solution.py:156
  65.4 2.0 %broadcast_select_fusion.9 = f32[256,512]{1,0:T(8,128)} fusion(f32[256,512]{1,0:T(8,128)} %collective-permute-done.6, f32[256,512]{1,0:T(8,128)S(1)} %broadcast_select_fusion.8, pred[]{:T(512)S(6)} %or.13), kind=kLoop, calls=%fused_computation.82 | loop fusion | flops 131072 | bytes 1572865 | tf_op jit(solution)/shard_map/jit(_where)/select_n | solution.py:157
  67.4 0.1 broadcast_select_fusion.1
  67.4 0.1 collective-permute-start.11
  67.6 1.9 %collective-permute-done.11 = f32[256,512]{1,0:T(8,128)S(1)} collective-permute-done((f32[256,512]{1,0:T(8,128)S(1)}, f32[256,512]{1,0:T(8,128)S(1)}, u32[]{:S(2)}, u32[]{:S(2)}) %collective-permute-start.11) | collective-permute-done | bytes 524320 | tf_op jit(solution)/shard_map/ppermute | solution.py:171
  69.4 0.1 broadcast_select_fusion
  69.7 1.5 %fusion.2.x_ref = f32[256,768]{1,0:T(8,128)S(1)} fusion(f32[256,512]{1,0:T(8,128)S(1)} %copy-done.11, f32[256,256]{1,0:T(8,128)S(1)} %broadcast_in_dim.3, f32[256,512]{1,0:T(8,128)S(1)} %get-tuple-element.86, f32[256,256]{1,0:T(8,128)S(1)} %get-tuple-element.84, f32[256,256]{1,0:T(8,128)S(1)} %get-tuple-element.83), kind=kOutput, calls=%fused_computation.5 | convolution fusion | flops 1209925632 | bytes 2621440 | tf_op jit(solution)/shard_map/dot_general | solution.py:181
  71.2 0.6 fusion.32
  71.9 0.6 fusion.34
  72.5 0.1 slice_subtract_fusion.2
  72.6 0.7 copy-done.3
  73.4 0.9 fusion.43
  74.2 1.3 collective-permute-start.12
  75.5 0.7 collective-permute-start.13
  76.2 1.5 %collective-permute-start.14 = (f32[256,512]{1,0:T(8,128)}, f32[256,512]{1,0:T(8,128)}, u32[]{:S(2)}, u32[]{:S(2)}) collective-permute-start(f32[256,512]{1,0:T(8,128)} %fusion.43), channel_id=1, source_target_pairs={{32,0},{160,128},{64,96},{192,224},{33,1},{161,129},{65,97},{193,2... | collective-permute-start | bytes 1572872 | tf_op jit(solution)/shard_map/ppermute | solution.py:171
  77.7 7.0 %shard_map.76 = (f32[2048,256]{1,0:T(8,128)}, f32[2048,256]{1,0:T(8,128)}, f32[2048,256]{1,0:T(8,128)}) custom-call(s32[1]{0:T(128)} %bitcast.21.flag_ref, f32[256,768]{1,0:T(8,128)} %copy-done.2, f32[2048,256]{1,0:T(8,128)} %v_ref.1, f32[2048,256]{1,0:T(8,128)} %w_ref.1, f32[2048,256]{1,0:T(8,128)} %g_ref.1), custom_call_target="tpu_custom_call" | custom-call | tf_op jit(solution)/shard_map/pallas_call | solution.py:67
  84.8 0.7 collective-permute-done.12
  85.5 1.3 select_select_fusion.2
  86.9 1.5 %fusion.6.x_ref = f32[256,768]{1,0:T(8,128)S(1)} fusion(f32[256,512]{1,0:T(8,128)S(1)} %copy-done.10, f32[256,256]{1,0:T(8,128)S(1)} %broadcast_in_dim.3, f32[256,512]{1,0:T(8,128)S(1)} %get-tuple-element.38, f32[256,256]{1,0:T(8,128)S(1)} %get-tuple-element.78, f32[256,256]{1,0:T(8,128)S(1)} %get-tuple-element.77), kind=kOutput, calls=%fused_computation.8 | convolution fusion | flops 1209925632 | bytes 2621440 | tf_op jit(solution)/shard_map/dot_general | solution.py:181
  88.4 0.6 fusion.30
  89.0 0.6 fusion.38
  89.7 0.1 slice_subtract_fusion
  89.7 0.1 slice_subtract_fusion.1
  89.8 0.9 fusion.42
  90.7 1.3 collective-permute-start.15
  92.0 0.7 collective-permute-start.16
  92.7 0.7 collective-permute-start.17
  93.4 0.7 collective-permute-start.18
  94.1 1.5 %collective-permute-start.19 = (f32[256,512]{1,0:T(8,128)}, f32[256,512]{1,0:T(8,128)}, u32[]{:S(2)}, u32[]{:S(2)}) collective-permute-start(f32[256,512]{1,0:T(8,128)} %fusion.42), channel_id=1, source_target_pairs={{96,64},{128,160},{97,65},{129,161},{98,66},{130,162},{99,67},{131... | collective-permute-start | bytes 1572872 | tf_op jit(solution)/shard_map/ppermute | solution.py:171
  95.6 7.9 %collective-permute-done.15 = f32[256,512]{1,0:T(8,128)S(1)} collective-permute-done((f32[256,512]{1,0:T(8,128)}, f32[256,512]{1,0:T(8,128)S(1)}, u32[]{:S(2)}, u32[]{:S(2)}) %collective-permute-start.15) | collective-permute-done | bytes 524320 | tf_op jit(solution)/shard_map/ppermute | solution.py:171
  103.5 1.5 %collective-permute-start.20 = (f32[256,512]{1,0:T(8,128)}, f32[256,512]{1,0:T(8,128)}, u32[]{:S(2)}, u32[]{:S(2)}) collective-permute-start(f32[256,512]{1,0:T(8,128)} %fusion.42), channel_id=1, source_target_pairs={{96,32},{128,192},{97,33},{129,193},{98,34},{130,194},{99,35},{131... | collective-permute-start | bytes 1572872 | tf_op jit(solution)/shard_map/ppermute | solution.py:171
  104.9 1.3 collective-permute-start.21
  106.2 6.9 %shard_map.77 = (f32[2048,256]{1,0:T(8,128)}, f32[2048,256]{1,0:T(8,128)}, f32[2048,256]{1,0:T(8,128)}) custom-call(s32[1]{0:T(128)} %bitcast.22.flag_ref, f32[256,768]{1,0:T(8,128)} %copy-done.1, f32[2048,256]{1,0:T(8,128)} %get-tuple-element.40.v_ref, f32[2048,256]{1,0:T(8,128)} %get-tuple-element.41.w_ref, f32[2048,256]{1,0:T(8,128)} %get-tuple-element.42.g_ref), custom_call_target="tpu_custom_call" | custom-call | tf_op jit(solution)/shard_map/pallas_call | solution.py:67
  113.2 7.8 %collective-permute-done.21 = f32[256,512]{1,0:T(8,128)} collective-permute-done((f32[256,512]{1,0:T(8,128)}, f32[256,512]{1,0:T(8,128)}, u32[]{:S(2)}, u32[]{:S(2)}) %collective-permute-start.21) | collective-permute-done | bytes 524320 | tf_op jit(solution)/shard_map/ppermute | solution.py:171
  121.0 1.9 %select_select_fusion = (f32[256,512]{1,0:T(8,128)S(1)}, f32[256,512]{1,0:T(8,128)S(1)}) fusion(f32[256,512]{1,0:T(8,128)S(1)} %collective-permute-done.15, f32[256,512]{1,0:T(8,128)S(1)} %collective-permute-done.16, f32[256,512]{1,0:T(8,128)S(1)} %collective-permute-done.17, f32[256,512]{1,0:T(8,128)S(1)} %collective-permute-done.18, ...), kind=kLoop, calls=%fused_computation.49 | loop fusion | flops 2097152 | bytes 5767176 | tf_op jit(solution)/shard_map/jit(_where)/select_n | solution.py:173
  123.0 2.4 %fusion.10.x_ref = f32[256,768]{1,0:T(8,128)} fusion(f32[256,512]{1,0:T(8,128)S(1)} %copy-done.9, f32[256,256]{1,0:T(8,128)S(1)} %copy-done.13, f32[256,512]{1,0:T(8,128)S(1)} %get-tuple-element.46, f32[256,256]{1,0:T(8,128)S(1)} %get-tuple-element.72, f32[256,256]{1,0:T(8,128)S(1)} %get-tuple-element.71), kind=kOutput, calls=%fused_computation.11 | convolution fusion | flops 1209925632 | bytes 2621440 | tf_op jit(solution)/shard_map/dot_general | solution.py:181
  125.3 6.9 %shard_map.78 = (f32[2048,256]{1,0:T(8,128)}, f32[2048,256]{1,0:T(8,128)}, f32[2048,256]{1,0:T(8,128)}) custom-call(s32[1]{0:T(128)} %bitcast.flag_ref, f32[256,768]{1,0:T(8,128)} %fusion.10.x_ref, f32[2048,256]{1,0:T(8,128)} %get-tuple-element.48.v_ref, f32[2048,256]{1,0:T(8,128)} %get-tuple-element.49.w_ref, f32[2048,256]{1,0:T(8,128)} %get-tuple-element.50.g_ref), custom_call_target="tpu_custom_call" | custom-call | tf_op jit(solution)/shard_map/pallas_call | solution.py:67
  (48 shorter events, 0.3 us)
Async XLA Ops:
  0.6 3.2 %copy-start.14 = (s32[9,2,32]{2,1,0:T(2,128)S(1)}, s32[9,2,32]{2,1,0:T(2,128)}, u32[]{:S(2)}) copy-start(s32[9,2,32]{2,1,0:T(2,128)} %constant.82.clone) | copy-start | bytes 6916
  2.7 8.5 %copy-start.7 = (f32[256,256]{1,0:T(8,128)}, f32[256,256]{1,0:T(8,128)S(1)}, u32[]{:S(2)}) copy-start(f32[256,256]{1,0:T(8,128)S(1)} %get-tuple-element.57) | copy-start | bytes 786436
  5.2 5.9 %collective-permute-start.1 = (f32[256,512]{1,0:T(8,128)S(1)}, f32[256,512]{1,0:T(8,128)S(1)}, u32[]{:S(2)}, u32[]{:S(2)}) collective-permute-start(f32[256,512]{1,0:T(8,128)S(1)} %fusion.44), channel_id=1, source_target_pairs={{0,16},{31,15},{64,80},{95,79},{128,144},{159,143},{192,208},{223,... | collective-permute-start | bytes 1572872 | tf_op jit(solution)/shard_map/ppermute | solution.py:123
  5.9 5.2 %collective-permute-start.2 = (f32[256,512]{1,0:T(8,128)S(1)}, f32[256,512]{1,0:T(8,128)S(1)}, u32[]{:S(2)}, u32[]{:S(2)}) collective-permute-start(f32[256,512]{1,0:T(8,128)S(1)} %fusion.44), channel_id=1, source_target_pairs={{0,24},{31,7},{64,88},{95,71},{128,152},{159,135},{192,216},{223,1... | collective-permute-start | bytes 1572872 | tf_op jit(solution)/shard_map/ppermute | solution.py:123
  6.6 4.5 %collective-permute-start = (f32[256,512]{1,0:T(8,128)S(1)}, f32[256,512]{1,0:T(8,128)S(1)}, u32[]{:S(2)}, u32[]{:S(2)}) collective-permute-start(f32[256,512]{1,0:T(8,128)S(1)} %fusion.44), channel_id=1, source_target_pairs={{0,8},{31,23},{64,72},{95,87},{128,136},{159,151},{192,200},{223,2... | collective-permute-start | bytes 1572872 | tf_op jit(solution)/shard_map/ppermute | solution.py:123
  11.2 1.5 %copy-start = (f32[1,3,256,512]{3,2,1,0:T(8,128)S(1)}, f32[1,3,256,512]{3,2,1,0:T(8,128)}, u32[]{:S(2)}) copy-start(f32[1,3,256,512]{3,2,1,0:T(8,128)} %param.8) | copy-start | bytes 4718596
  13.8 7.8 %collective-permute-start.4 = (f32[256,512]{1,0:T(8,128)}, f32[256,512]{1,0:T(8,128)}, u32[]{:S(2)}, u32[]{:S(2)}) collective-permute-start(f32[256,512]{1,0:T(8,128)} %get-tuple-element.62), channel_id=1, source_target_pairs={{96,64},{128,160},{97,65},{129,161},{98,66},{130,162},{99,67},{131... | collective-permute-start | bytes 1572872 | tf_op jit(solution)/shard_map/ppermute | solution.py:156
  15.3 6.3 %collective-permute-start.3 = (f32[256,512]{1,0:T(8,128)}, f32[256,512]{1,0:T(8,128)}, u32[]{:S(2)}, u32[]{:S(2)}) collective-permute-start(f32[256,512]{1,0:T(8,128)} %get-tuple-element.63), channel_id=1, source_target_pairs={{32,0},{160,128},{64,96},{192,224},{33,1},{161,129},{65,97},{193,2... | collective-permute-start | bytes 1572872 | tf_op jit(solution)/shard_map/ppermute | solution.py:156
  18.1 10.8 %collective-permute-start.8 = (f32[256,512]{1,0:T(8,128)}, f32[256,512]{1,0:T(8,128)S(1)}, u32[]{:S(2)}, u32[]{:S(2)}) collective-permute-start(f32[256,512]{1,0:T(8,128)} %broadcast_select_fusion.5), channel_id=1, source_target_pairs={{0,2},{8,10},{16,18},{24,26},{7,5},{23,21},{15,13},{31,29},{64,66}... | collective-permute-start | bytes 1572872 | tf_op jit(solution)/shard_map/ppermute | solution.py:123
  18.8 23.7 %collective-permute-start.9 = (f32[256,512]{1,0:T(8,128)}, f32[256,512]{1,0:T(8,128)}, u32[]{:S(2)}, u32[]{:S(2)}) collective-permute-start(f32[256,512]{1,0:T(8,128)} %broadcast_select_fusion.5), channel_id=1, source_target_pairs={{0,3},{8,11},{16,19},{24,27},{7,4},{23,20},{15,12},{31,28},{64,67}... | collective-permute-start | bytes 1572872 | tf_op jit(solution)/shard_map/ppermute | solution.py:123
  20.1 22.4 %collective-permute-start.7 = (f32[256,512]{1,0:T(8,128)}, f32[256,512]{1,0:T(8,128)}, u32[]{:S(2)}, u32[]{:S(2)}) collective-permute-start(f32[256,512]{1,0:T(8,128)} %broadcast_select_fusion.5), channel_id=1, source_target_pairs={{0,1},{8,9},{16,17},{24,25},{7,6},{23,22},{15,14},{31,30},{64,65},... | collective-permute-start | bytes 1572872 | tf_op jit(solution)/shard_map/ppermute | solution.py:123
  23.8 25.5 %collective-permute-start.5 = (f32[256,512]{1,0:T(8,128)}, f32[256,512]{1,0:T(8,128)S(1)}, u32[]{:S(2)}, u32[]{:S(2)}) collective-permute-start(f32[256,512]{1,0:T(8,128)} %get-tuple-element.60), channel_id=1, source_target_pairs={{96,32},{128,192},{97,33},{129,193},{98,34},{130,194},{99,35},{131... | collective-permute-start | bytes 1572872 | tf_op jit(solution)/shard_map/ppermute | solution.py:156
  28.9 13.6 %copy-start.8 = (f32[256,512]{1,0:T(8,128)}, f32[256,512]{1,0:T(8,128)S(1)}, u32[]{:S(2)}) copy-start(f32[256,512]{1,0:T(8,128)S(1)} %collective-permute-done.8) | copy-start | bytes 1572868
  44.2 13.7 %collective-permute-start.10 = (f32[256,512]{1,0:T(8,128)S(1)}, f32[256,512]{1,0:T(8,128)S(1)}, u32[]{:S(2)}, u32[]{:S(2)}) collective-permute-start(f32[256,512]{1,0:T(8,128)S(1)} %get-tuple-element.51), channel_id=1, source_target_pairs={{0,4},{1,5},{2,6},{3,7},{8,12},{9,13},{10,14},{11,15},{16,20},{17,... | collective-permute-start | bytes 1572872 | tf_op jit(solution)/shard_map/ppermute | solution.py:123
  50.5 14.9 %collective-permute-start.6 = (f32[256,512]{1,0:T(8,128)S(1)}, f32[256,512]{1,0:T(8,128)}, u32[]{:S(2)}, u32[]{:S(2)}) collective-permute-start(f32[256,512]{1,0:T(8,128)S(1)} %broadcast_select_fusion.8), channel_id=1, source_target_pairs={{96,0},{128,224},{97,1},{129,225},{98,2},{130,226},{99,3},{131,227... | collective-permute-start | bytes 1572872 | tf_op jit(solution)/shard_map/ppermute | solution.py:156
  67.4 2.0 %collective-permute-start.11 = (f32[256,512]{1,0:T(8,128)S(1)}, f32[256,512]{1,0:T(8,128)S(1)}, u32[]{:S(2)}, u32[]{:S(2)}) collective-permute-start(f32[256,512]{1,0:T(8,128)S(1)} %broadcast_select_fusion.1), channel_id=1, source_target_pairs={{0,32},{64,96},{128,160},{192,224},{32,0},{96,64},{160,128},{224,1... | collective-permute-start | bytes 1572872 | tf_op jit(solution)/shard_map/ppermute | solution.py:171
  67.6 2.1 %copy-start.11 = (f32[256,512]{1,0:T(8,128)S(1)}, f32[256,512]{1,0:T(8,128)}, u32[]{:S(2)}) copy-start(f32[256,512]{1,0:T(8,128)} %get-tuple-element.32) | copy-start | bytes 1572868
  69.7 17.2 %copy-start.12 = (f32[256,256]{1,0:T(8,128)}, f32[256,256]{1,0:T(8,128)S(1)}, u32[]{:S(2)}) copy-start(f32[256,256]{1,0:T(8,128)S(1)} %broadcast_in_dim.3) | copy-start | bytes 786436
  71.2 1.3 copy-start.2
  72.6 0.7 copy-start.3
  72.6 1.6 %copy-start.5 = (f32[256,256]{1,0:T(8,128)}, f32[256,256]{1,0:T(8,128)S(1)}, u32[]{:S(2)}) copy-start(f32[256,256]{1,0:T(8,128)S(1)} %get-tuple-element.98) | copy-start | bytes 786436
  74.2 11.3 %collective-permute-start.12 = (f32[256,512]{1,0:T(8,128)}, f32[256,512]{1,0:T(8,128)S(1)}, u32[]{:S(2)}, u32[]{:S(2)}) collective-permute-start(f32[256,512]{1,0:T(8,128)} %fusion.43), channel_id=1, source_target_pairs={{32,96},{160,224},{64,0},{192,128},{33,97},{161,225},{65,1},{193,1... | collective-permute-start | bytes 1572872 | tf_op jit(solution)/shard_map/ppermute | solution.py:171
  75.5 10.0 %collective-permute-start.13 = (f32[256,512]{1,0:T(8,128)}, f32[256,512]{1,0:T(8,128)S(1)}, u32[]{:S(2)}, u32[]{:S(2)}) collective-permute-start(f32[256,512]{1,0:T(8,128)} %fusion.43), channel_id=1, source_target_pairs={{32,64},{160,192},{64,32},{192,160},{33,65},{161,193},{65,33},{193... | collective-permute-start | bytes 1572872 | tf_op jit(solution)/shard_map/ppermute | solution.py:171
  76.2 9.3 %collective-permute-start.14 = (f32[256,512]{1,0:T(8,128)}, f32[256,512]{1,0:T(8,128)}, u32[]{:S(2)}, u32[]{:S(2)}) collective-permute-start(f32[256,512]{1,0:T(8,128)} %fusion.43), channel_id=1, source_target_pairs={{32,0},{160,128},{64,96},{192,224},{33,1},{161,129},{65,97},{193,2... | collective-permute-start | bytes 1572872 | tf_op jit(solution)/shard_map/ppermute | solution.py:171
  77.7 7.8 %copy-start.4 = (f32[256,256]{1,0:T(8,128)S(1)}, f32[256,256]{1,0:T(8,128)}, u32[]{:S(2)}) copy-start(f32[256,256]{1,0:T(8,128)} %copy-done.3) | copy-start | bytes 786436
  77.7 7.8 %copy-start.6 = (f32[256,256]{1,0:T(8,128)S(1)}, f32[256,256]{1,0:T(8,128)}, u32[]{:S(2)}) copy-start(f32[256,256]{1,0:T(8,128)} %copy-done.5) | copy-start | bytes 786436
  84.8 2.1 %copy-start.10 = (f32[256,512]{1,0:T(8,128)S(1)}, f32[256,512]{1,0:T(8,128)}, u32[]{:S(2)}) copy-start(f32[256,512]{1,0:T(8,128)} %get-tuple-element.34) | copy-start | bytes 1572868
  88.4 1.3 copy-start.1
  90.7 12.8 %collective-permute-start.15 = (f32[256,512]{1,0:T(8,128)}, f32[256,512]{1,0:T(8,128)S(1)}, u32[]{:S(2)}, u32[]{:S(2)}) collective-permute-start(f32[256,512]{1,0:T(8,128)} %fusion.42), channel_id=1, source_target_pairs={{96,224},{128,0},{97,225},{129,1},{98,226},{130,2},{99,227},{131,3... | collective-permute-start | bytes 1572872 | tf_op jit(solution)/shard_map/ppermute | solution.py:171
  92.0 12.9 %collective-permute-start.16 = (f32[256,512]{1,0:T(8,128)}, f32[256,512]{1,0:T(8,128)S(1)}, u32[]{:S(2)}, u32[]{:S(2)}) collective-permute-start(f32[256,512]{1,0:T(8,128)} %fusion.42), channel_id=1, source_target_pairs={{96,192},{128,32},{97,193},{129,33},{98,194},{130,34},{99,195},{13... | collective-permute-start | bytes 1572872 | tf_op jit(solution)/shard_map/ppermute | solution.py:171
  92.7 20.5 %collective-permute-start.17 = (f32[256,512]{1,0:T(8,128)}, f32[256,512]{1,0:T(8,128)S(1)}, u32[]{:S(2)}, u32[]{:S(2)}) collective-permute-start(f32[256,512]{1,0:T(8,128)} %fusion.42), channel_id=1, source_target_pairs={{96,160},{128,64},{97,161},{129,65},{98,162},{130,66},{99,163},{13... | collective-permute-start | bytes 1572872 | tf_op jit(solution)/shard_map/ppermute | solution.py:171
  93.4 19.8 %collective-permute-start.18 = (f32[256,512]{1,0:T(8,128)}, f32[256,512]{1,0:T(8,128)S(1)}, u32[]{:S(2)}, u32[]{:S(2)}) collective-permute-start(f32[256,512]{1,0:T(8,128)} %fusion.42), channel_id=1, source_target_pairs={{96,128},{128,96},{97,129},{129,97},{98,130},{130,98},{99,131},{13... | collective-permute-start | bytes 1572872 | tf_op jit(solution)/shard_map/ppermute | solution.py:171
  94.1 19.1 %collective-permute-start.19 = (f32[256,512]{1,0:T(8,128)}, f32[256,512]{1,0:T(8,128)}, u32[]{:S(2)}, u32[]{:S(2)}) collective-permute-start(f32[256,512]{1,0:T(8,128)} %fusion.42), channel_id=1, source_target_pairs={{96,64},{128,160},{97,65},{129,161},{98,66},{130,162},{99,67},{131... | collective-permute-start | bytes 1572872 | tf_op jit(solution)/shard_map/ppermute | solution.py:171
  103.5 9.7 %collective-permute-start.20 = (f32[256,512]{1,0:T(8,128)}, f32[256,512]{1,0:T(8,128)}, u32[]{:S(2)}, u32[]{:S(2)}) collective-permute-start(f32[256,512]{1,0:T(8,128)} %fusion.42), channel_id=1, source_target_pairs={{96,32},{128,192},{97,33},{129,193},{98,34},{130,194},{99,35},{131... | collective-permute-start | bytes 1572872 | tf_op jit(solution)/shard_map/ppermute | solution.py:171
  104.9 16.1 %collective-permute-start.21 = (f32[256,512]{1,0:T(8,128)}, f32[256,512]{1,0:T(8,128)}, u32[]{:S(2)}, u32[]{:S(2)}) collective-permute-start(f32[256,512]{1,0:T(8,128)} %fusion.42), channel_id=1, source_target_pairs={{96,0},{128,224},{97,1},{129,225},{98,2},{130,226},{99,3},{131,227... | collective-permute-start | bytes 1572872 | tf_op jit(solution)/shard_map/ppermute | solution.py:171
  113.2 9.8 %copy-start.9 = (f32[256,512]{1,0:T(8,128)S(1)}, f32[256,512]{1,0:T(8,128)}, u32[]{:S(2)}) copy-start(f32[256,512]{1,0:T(8,128)} %broadcast_select_fusion.9) | copy-start | bytes 1572868
  113.2 9.8 %copy-start.13 = (f32[256,256]{1,0:T(8,128)S(1)}, f32[256,256]{1,0:T(8,128)}, u32[]{:S(2)}) copy-start(f32[256,256]{1,0:T(8,128)} %copy-done.12) | copy-start | bytes 786436

commit v2 on v0

--- a/solution.py
+++ b/solution.py
@@ -155,7 +155,6 @@
     else:
         top, bottom = spread_tips(first_tip, last_tip, row_pos, row_count, row_fanouts(row_count))
     inverses, top, bottom = lax.optimization_barrier((inverses, top, bottom))
-    blank_block = jnp.zeros((band, band), jnp.float32)
     for level in range(LEVELS):
         half = 2**level
         place = chain_pos % (2 * half)
@@ -173,10 +172,14 @@
             lower_tip, upper_tip, spike_right, spike_left, load_block = lax.optimization_barrier(
                 (lower_tip, upper_tip, spike_right, spike_left, load_block)
             )
-        upper_rows = jnp.concatenate([lower_tip[:, :band], lower_tip[:, band:], blank_block], 1)
-        lower_rows = jnp.concatenate([upper_tip[:, :band], blank_block, upper_tip[:, band:]], 1)
-        tip_rhs = jnp.concatenate([upper_rows, lower_rows], 0)
-        solved = jnp.dot(inverses[level], tip_rhs, precision=precise, preferred_element_type=jnp.float32)
+        inverse_low = inverses[level][:, :band]
+        inverse_up = inverses[level][:, band:]
+        solved_load = jnp.dot(
+            inverse_low, lower_tip[:, :band], precision=precise, preferred_element_type=jnp.float32
+        ) + jnp.dot(inverse_up, upper_tip[:, :band], precision=precise, preferred_element_type=jnp.float32)
+        solved_left = jnp.dot(inverse_low, lower_tip[:, band:], precision=precise, preferred_element_type=jnp.float32)
+        solved_right = jnp.dot(inverse_up, upper_tip[:, band:], precision=precise, preferred_element_type=jnp.float32)
+        solved = jnp.concatenate([solved_load, solved_left, solved_right], 1)
         if level + 1 < LEVELS:
             bottom_prod = jnp.dot(
                 bottom[:, band:], solved[:, : 2 * band], precision=precise, preferred_element_type=jnp.float32

time: 132 us -> 139 us (1.053)
  other arithmetic: 13.8 us -> 21.8 us
  waiting for transfers between devices: 36 us -> 32.2 us
  starting transfers between devices: 34.8 us -> 36.3 us
    concatenate x0 -> x3, other arithmetic: none -> 3.83 us  [on_device(): solved = jnp.concatenate([solved_load, solved_left, solved_right], 1)]
    ppermute x11, waiting for transfers between devices: 22.3 us -> 19.4 us  [on_device(): got = lax.ppermute(sent, 'chain', pairs)]
    select_n x3, other arithmetic: 1.07 us -> 2.71 us  [on_device(): sent = jnp.where(place == half - 1, bottom, top)]
    unnamed x18 -> x26, local copies, waits for them, and re-layouts: 0.04 us -> 1.56 us
    ppermute x11, starting transfers between devices: 11.9 us -> 13.4 us  [on_device(): got = lax.ppermute(sent, 'chain', pairs)]
    dot_general x3 -> x12, matrix products: 5.32 us -> 4.56 us  [the longest x3 1.14 us: on_device(): jnp.dot(inverse_up, upper_tip[:, :band], precision=precise, preferred_ele...]
    select_n x3 -> x2, other arithmetic: 3.46 us -> 3.63 us  [on_device(): upper_tip = jnp.where(place == half - offset, got, upper_tip)]
  transfers between devices with their start and end apart: 22 -> 22, of which waited for: 8 -> 8; matrix products, arithmetic and copies ran while one was open for 10% -> 12% of each run, Pallas kernels for 11% -> 10%
where the time goes in v2:
time: 139 us; the launch traced here: 138 us
  starting transfers between devices  36.3 us (26%)
  waiting for transfers between devices  32.2 us (23%)
  other arithmetic  21.8 us (16%)
  Pallas kernels  20.8 us (15%)
  between operations  11.8 us (8%)
  local copies, waits for them, and re-layouts  7.73 us (6%)
  matrix products  7.03 us (5%)
    pallas_call x3, Pallas kernels, bulk_update(): pl.pallas_call(bulk_kernel, grid_spec=pltpu.PrefetchScalarGridSpec(num_sc...  20.8 us
    ppermute x11, waiting for transfers between devices, on_device(): got = lax.ppermute(sent, 'chain', pairs)  19.4 us
    ppermute x7, starting transfers between devices, core_tree(): lax.ppermute(sent, ('chain', 'rows'), pairs)  18 us
    ppermute x11, starting transfers between devices, on_device(): got = lax.ppermute(sent, 'chain', pairs)  13.4 us
    ppermute x7, waiting for transfers between devices, core_tree(): lax.ppermute(sent, ('chain', 'rows'), pairs)  12.8 us
    select_n x3, other arithmetic, core_tree(): sent = jnp.where(mine[3 * step + 2] == 1, top, bottom)  5.78 us
    ppermute x4, starting transfers between devices, on_device(): got = lax.ppermute(mine, 'chain', pairs)  4.86 us
    select_n x3, other arithmetic, on_device(): mine = jnp.where((place == half - 1 - k) | (place == half + k), got, mine)  4.31 us
  transfers between devices with their start and end apart: 22, of which 8 were waited for; matrix products, arithmetic and copies ran while one was open for 12% of the time, Pallas kernels for 10%

profile of v2, /device:TPU:31, one launch (start us, length us, event | category | flops | bytes accessed | tf_op | source)
XLA Modules:
  0.0 137.8 jit_solution(18043709561330226638)
XLA Ops:
  0.6 2.4 %slice_bitcast_fusion = (f32[256,512]{1,0:T(8,128)}, f32[256,512]{1,0:T(8,128)S(1)}, f32[256,512]{1,0:T(8,128)}) fusion(f32[1,3,256,512]{3,2,1,0:T(8,128)} %param.8), kind=kLoop, calls=%fused_computation.32 | loop fusion | bytes 3145728 | tf_op jit(solution)/shard_map/squeeze | solution.py:145
  3.1 0.8 collective-permute-start.1
  3.9 1.3 collective-permute-start
  5.2 1.0 slice.161
  6.2 1.0 slice.158
  7.2 0.7 fusion.51
  8.6 1.1 fusion.50
  9.6 0.7 copy-done.9
  10.4 0.9 fusion.10
  11.2 1.5 %collective-permute-start.5 = (f32[256,512]{1,0:T(8,128)}, f32[256,512]{1,0:T(8,128)}, u32[]{:S(2)}, u32[]{:S(2)}) collective-permute-start(f32[256,512]{1,0:T(8,128)} %fusion.10), channel_id=1, source_target_pairs={{0,16},{31,15},{64,80},{95,79},{128,144},{159,143},{192,208},{223,... | collective-permute-start | bytes 1572872 | tf_op jit(solution)/shard_map/ppermute | solution.py:123
  12.7 1.3 collective-permute-start.6
  14.0 1.5 %collective-permute-start.4 = (f32[256,512]{1,0:T(8,128)}, f32[256,512]{1,0:T(8,128)}, u32[]{:S(2)}, u32[]{:S(2)}) collective-permute-start(f32[256,512]{1,0:T(8,128)} %fusion.10), channel_id=1, source_target_pairs={{0,8},{31,23},{64,72},{95,87},{128,136},{159,151},{192,200},{223,2... | collective-permute-start | bytes 1572872 | tf_op jit(solution)/shard_map/ppermute | solution.py:123
  19.7 0.8 copy-done.11
  20.5 2.0 %broadcast_select_fusion.7 = (f32[256,512]{1,0:T(8,128)}, f32[256,512]{1,0:T(8,128)S(1)}) fusion(f32[256,512]{1,0:T(8,128)} %copy-done.11, pred[]{:T(512)S(6)} %or.15, f32[1,3,256,512]{3,2,1,0:T(8,128)S(1)} %copy-done, f32[256,512]{1,0:T(8,128)} %collective-permute-done, pred[]{:T(512)S(6)} %or.12), kind=kLoop, calls=%fused_computation.76 | loop fusion | flops 262144 | bytes 3145730 | tf_op jit(solution)/shard_map/jit(_where)/select_n | solution.py:149
  22.5 1.5 %collective-permute-start.2 = (f32[256,512]{1,0:T(8,128)}, f32[256,512]{1,0:T(8,128)}, u32[]{:S(2)}, u32[]{:S(2)}) collective-permute-start(f32[256,512]{1,0:T(8,128)} %get-tuple-element.57), channel_id=1, source_target_pairs={{96,32},{128,192},{97,33},{129,193},{98,34},{130,194},{99,35},{131... | collective-permute-start | bytes 1572872 | tf_op jit(solution)/shard_map/ppermute | solution.py:148
  24.0 1.0 collective-permute-done.6
  25.0 2.4 %broadcast_select_fusion.5 = (f32[256,512]{1,0:T(8,128)}, f32[256,512]{1,0:T(8,128)S(1)}, f32[256,512]{1,0:T(8,128)S(1)}) fusion(pred[]{:T(512)} %bitcast.11, f32[256,512]{1,0:T(8,128)} %collective-permute-done.5, f32[256,512]{1,0:T(8,128)} %collective-permute-done.6, pred[]{:T(512)} %bitcast.14, f32[256,512]{1,0:T(8,128)} %collective-permute-done.4, ...), kind=kLoop, calls=%fused_computation.74 | loop fusion | flops 1179648 | bytes 4194311 | tf_op jit(solution)/shard_map/jit(_where)/select_n | solution.py:122
  27.4 8.1 %collective-permute-start.8 = (f32[256,512]{1,0:T(8,128)}, f32[256,512]{1,0:T(8,128)S(1)}, u32[]{:S(2)}, u32[]{:S(2)}) collective-permute-start(f32[256,512]{1,0:T(8,128)} %get-tuple-element.48), channel_id=1, source_target_pairs={{0,2},{8,10},{16,18},{24,26},{7,5},{23,21},{15,13},{31,29},{64,66}... | collective-permute-start | bytes 1572872 | tf_op jit(solution)/shard_map/ppermute | solution.py:123
  35.5 2.1 %collective-permute-start.9 = (f32[256,512]{1,0:T(8,128)}, f32[256,512]{1,0:T(8,128)}, u32[]{:S(2)}, u32[]{:S(2)}) collective-permute-start(f32[256,512]{1,0:T(8,128)} %get-tuple-element.48), channel_id=1, source_target_pairs={{0,3},{8,11},{16,19},{24,27},{7,4},{23,20},{15,12},{31,28},{64,67}... | collective-permute-start | bytes 1572872 | tf_op jit(solution)/shard_map/ppermute | solution.py:123
  37.6 2.1 %collective-permute-start.7 = (f32[256,512]{1,0:T(8,128)}, f32[256,512]{1,0:T(8,128)}, u32[]{:S(2)}, u32[]{:S(2)}) collective-permute-start(f32[256,512]{1,0:T(8,128)} %get-tuple-element.48), channel_id=1, source_target_pairs={{0,1},{8,9},{16,17},{24,25},{7,6},{23,22},{15,14},{31,30},{64,65},... | collective-permute-start | bytes 1572872 | tf_op jit(solution)/shard_map/ppermute | solution.py:123
  44.3 1.1 broadcast_select_fusion.8
  45.4 1.3 collective-permute-start.3
  46.7 0.7 collective-permute-done.8
  47.5 5.6 %collective-permute-done.7 = f32[256,512]{1,0:T(8,128)} collective-permute-done((f32[256,512]{1,0:T(8,128)}, f32[256,512]{1,0:T(8,128)}, u32[]{:S(2)}, u32[]{:S(2)}) %collective-permute-start.7) | collective-permute-done | bytes 524320 | tf_op jit(solution)/shard_map/ppermute | solution.py:123
  53.1 2.5 %broadcast_select_fusion.4 = (f32[256,512]{1,0:T(8,128)}, f32[256,512]{1,0:T(8,128)}, f32[256,512]{1,0:T(8,128)}) fusion(pred[]{:T(512)} %bitcast.16, f32[256,512]{1,0:T(8,128)S(1)} %collective-permute-done.8, f32[256,512]{1,0:T(8,128)} %collective-permute-done.9, pred[]{:T(512)} %bitcast.19, f32[256,512]{1,0:T(8,128)S(1)} %get-tuple-element.49, ...), kind=kLoop, calls=%fused_computation.73 | loop fusion | flops 917504 | bytes 4194311 | tf_op jit(solution)/shard_map/jit(_where)/select_n | solution.py:122
  55.6 1.5 %collective-permute-start.10 = (f32[256,512]{1,0:T(8,128)}, f32[256,512]{1,0:T(8,128)S(1)}, u32[]{:S(2)}, u32[]{:S(2)}) collective-permute-start(f32[256,512]{1,0:T(8,128)} %get-tuple-element.45), channel_id=1, source_target_pairs={{0,4},{1,5},{2,6},{3,7},{8,12},{9,13},{10,14},{11,15},{16,20},{17,... | collective-permute-start | bytes 1572872 | tf_op jit(solution)/shard_map/ppermute | solution.py:123
  58.4 1.1 broadcast_select_fusion.9
  59.5 5.5 %collective-permute-done.10 = f32[256,512]{1,0:T(8,128)S(1)} collective-permute-done((f32[256,512]{1,0:T(8,128)}, f32[256,512]{1,0:T(8,128)S(1)}, u32[]{:S(2)}, u32[]{:S(2)}) %collective-permute-start.10) | collective-permute-done | bytes 524320 | tf_op jit(solution)/shard_map/ppermute | solution.py:123
  65.0 1.2 broadcast_select_fusion.3
  66.2 0.9 broadcast_select_fusion.1
  67.1 2.1 %collective-permute-done.11 = f32[256,512]{1,0:T(8,128)S(1)} collective-permute-done((f32[256,512]{1,0:T(8,128)}, f32[256,512]{1,0:T(8,128)S(1)}, u32[]{:S(2)}, u32[]{:S(2)}) %collective-permute-start.11) | collective-permute-done | bytes 524320 | tf_op jit(solution)/shard_map/ppermute | solution.py:168
  70.2 0.4 fusion.13
  70.6 0.4 convolution_add_fusion.2
  70.9 0.6 fusion.3
  71.6 0.6 fusion.2
  72.4 0.9 fusion.9
  73.3 1.3 collective-permute-start.12
  74.6 1.5 %collective-permute-start.13 = (f32[256,512]{1,0:T(8,128)}, f32[256,512]{1,0:T(8,128)}, u32[]{:S(2)}, u32[]{:S(2)}) collective-permute-start(f32[256,512]{1,0:T(8,128)} %fusion.9), channel_id=1, source_target_pairs={{32,64},{160,192},{64,32},{192,160},{33,65},{161,193},{65,33},{193... | collective-permute-start | bytes 1572872 | tf_op jit(solution)/shard_map/ppermute | solution.py:168
  76.1 1.3 collective-permute-start.14
  77.4 2.0 %pad_maximum_fusion.x_ref = f32[256,768]{1,0:T(8,128)} fusion(f32[256,256]{1,0:T(8,128)} %copy-done.7, f32[256,256]{1,0:T(8,128)} %copy-done.8, f32[256,256]{1,0:T(8,128)S(1)} %convolution_add_fusion.2), kind=kLoop, calls=%fused_computation.3 | loop fusion | flops 393216 | bytes 1572864 | tf_op jit(solution)/shard_map/concatenate | solution.py:182
  79.4 7.0 %shard_map.76 = (f32[2048,256]{1,0:T(8,128)}, f32[2048,256]{1,0:T(8,128)}, f32[2048,256]{1,0:T(8,128)}) custom-call(s32[1]{0:T(128)} %bitcast.21.flag_ref, f32[256,768]{1,0:T(8,128)} %pad_maximum_fusion.x_ref, f32[2048,256]{1,0:T(8,128)} %v_ref.1, f32[2048,256]{1,0:T(8,128)} %w_ref.1, f32[2048,256]{1,0:T(8,128)} %g_ref.1), custom_call_target="tpu_custom_call" | custom-call | tf_op jit(solution)/shard_map/pallas_call | solution.py:67
  86.4 1.5 %collective-permute-done.12 = f32[256,512]{1,0:T(8,128)S(1)} collective-permute-done((f32[256,512]{1,0:T(8,128)}, f32[256,512]{1,0:T(8,128)S(1)}, u32[]{:S(2)}, u32[]{:S(2)}) %collective-permute-start.12) | collective-permute-done | bytes 524320 | tf_op jit(solution)/shard_map/ppermute | solution.py:168
  87.9 1.4 %select_select_fusion.2 = (f32[256,512]{1,0:T(8,128)S(1)}, f32[256,512]{1,0:T(8,128)S(1)}) fusion(f32[256,512]{1,0:T(8,128)S(1)} %collective-permute-done.12, f32[256,512]{1,0:T(8,128)} %collective-permute-done.13, f32[256,512]{1,0:T(8,128)} %collective-permute-done.14, f32[256,256]{1,0:T(8,128)S(1)} %copy-done.4, f32[256,256]{1,0:T(8,128)S(1)} %get-tuple-element.68, ...), kind=kLoop, calls=%fused_computation.26 | loop fusion | flops 1048576 | bytes 3670020 | tf_op jit(solution)/shard_map/jit(_where)/select_n | solution.py:170
  89.7 0.4 fusion.27
  90.1 0.4 fusion.25
  90.5 0.4 convolution_add_fusion.1
  90.9 0.6 fusion.1
  91.6 0.6 fusion
  92.3 0.9 fusion.8
  93.2 1.3 collective-permute-start.15
  94.5 0.9 collective-permute-start.16
  95.4 1.5 %collective-permute-start.17 = (f32[256,512]{1,0:T(8,128)}, f32[256,512]{1,0:T(8,128)}, u32[]{:S(2)}, u32[]{:S(2)}) collective-permute-start(f32[256,512]{1,0:T(8,128)} %fusion.8), channel_id=1, source_target_pairs={{96,160},{128,64},{97,161},{129,65},{98,162},{130,66},{99,163},{13... | collective-permute-start | bytes 1572872 | tf_op jit(solution)/shard_map/ppermute | solution.py:168
  96.9 1.5 %collective-permute-start.18 = (f32[256,512]{1,0:T(8,128)}, f32[256,512]{1,0:T(8,128)}, u32[]{:S(2)}, u32[]{:S(2)}) collective-permute-start(f32[256,512]{1,0:T(8,128)} %fusion.8), channel_id=1, source_target_pairs={{96,128},{128,96},{97,129},{129,97},{98,130},{130,98},{99,131},{13... | collective-permute-start | bytes 1572872 | tf_op jit(solution)/shard_map/ppermute | solution.py:168
  98.4 1.5 %collective-permute-start.19 = (f32[256,512]{1,0:T(8,128)}, f32[256,512]{1,0:T(8,128)}, u32[]{:S(2)}, u32[]{:S(2)}) collective-permute-start(f32[256,512]{1,0:T(8,128)} %fusion.8), channel_id=1, source_target_pairs={{96,64},{128,160},{97,65},{129,161},{98,66},{130,162},{99,67},{131... | collective-permute-start | bytes 1572872 | tf_op jit(solution)/shard_map/ppermute | solution.py:168
  99.8 5.0 %collective-permute-done.15 = f32[256,512]{1,0:T(8,128)S(1)} collective-permute-done((f32[256,512]{1,0:T(8,128)}, f32[256,512]{1,0:T(8,128)S(1)}, u32[]{:S(2)}, u32[]{:S(2)}) %collective-permute-start.15) | collective-permute-done | bytes 524320 | tf_op jit(solution)/shard_map/ppermute | solution.py:168
  104.8 1.4 %collective-permute-start.20 = (f32[256,512]{1,0:T(8,128)}, f32[256,512]{1,0:T(8,128)}, u32[]{:S(2)}, u32[]{:S(2)}) collective-permute-start(f32[256,512]{1,0:T(8,128)} %fusion.8), channel_id=1, source_target_pairs={{96,32},{128,192},{97,33},{129,193},{98,34},{130,194},{99,35},{131... | collective-permute-start | bytes 1572872 | tf_op jit(solution)/shard_map/ppermute | solution.py:168
  106.3 1.3 collective-permute-start.21
  107.6 0.9 pad_maximum_fusion.1.x_ref
  108.5 6.9 %shard_map.77 = (f32[2048,256]{1,0:T(8,128)}, f32[2048,256]{1,0:T(8,128)}, f32[2048,256]{1,0:T(8,128)}) custom-call(s32[1]{0:T(128)} %bitcast.22.flag_ref, f32[256,768]{1,0:T(8,128)} %pad_maximum_fusion.1.x_ref, f32[2048,256]{1,0:T(8,128)} %get-tuple-element.34.v_ref, f32[2048,256]{1,0:T(8,128)} %get-tuple-element.35.w_ref, f32[2048,256]{1,0:T(8,128)} %get-tuple-element.36.g_ref), custom_call_target="tpu_custom_call" | custom-call | tf_op jit(solution)/shard_map/pallas_call | solution.py:67
  115.4 10.8 %collective-permute-done.21 = f32[256,512]{1,0:T(8,128)} collective-permute-done((f32[256,512]{1,0:T(8,128)}, f32[256,512]{1,0:T(8,128)}, u32[]{:S(2)}, u32[]{:S(2)}) %collective-permute-start.21) | collective-permute-done | bytes 524320 | tf_op jit(solution)/shard_map/ppermute | solution.py:168
  126.2 2.2 %select_select_fusion = (f32[256,512]{1,0:T(8,128)S(1)}, f32[256,512]{1,0:T(8,128)S(1)}) fusion(f32[256,512]{1,0:T(8,128)S(1)} %collective-permute-done.15, f32[256,512]{1,0:T(8,128)S(1)} %collective-permute-done.16, f32[256,512]{1,0:T(8,128)} %collective-permute-done.17, f32[256,512]{1,0:T(8,128)} %collective-permute-done.18, ...), kind=kLoop, calls=%fused_computation.24 | loop fusion | flops 2097152 | bytes 5767176 | tf_op jit(solution)/shard_map/jit(_where)/select_n | solution.py:170
  129.5 0.4 convolution_add_fusion
  129.9 0.9 pad_maximum_fusion.2.x_ref
  130.9 6.9 %shard_map.78 = (f32[2048,256]{1,0:T(8,128)}, f32[2048,256]{1,0:T(8,128)}, f32[2048,256]{1,0:T(8,128)}) custom-call(s32[1]{0:T(128)} %bitcast.flag_ref, f32[256,768]{1,0:T(8,128)} %pad_maximum_fusion.2.x_ref, f32[2048,256]{1,0:T(8,128)} %get-tuple-element.42.v_ref, f32[2048,256]{1,0:T(8,128)} %get-tuple-element.43.w_ref, f32[2048,256]{1,0:T(8,128)} %get-tuple-element.44.g_ref), custom_call_target="tpu_custom_call" | custom-call | tf_op jit(solution)/shard_map/pallas_call | solution.py:67
  (49 shorter events, 2.8 us)
Async XLA Ops:
  0.6 6.6 %copy-start.12 = (s32[9,2,32]{2,1,0:T(2,128)S(1)}, s32[9,2,32]{2,1,0:T(2,128)}, u32[]{:S(2)}) copy-start(s32[9,2,32]{2,1,0:T(2,128)} %constant.80.clone) | copy-start | bytes 6916
  3.1 17.4 %copy-start = (f32[1,3,256,512]{3,2,1,0:T(8,128)S(1)}, f32[1,3,256,512]{3,2,1,0:T(8,128)}, u32[]{:S(2)}) copy-start(f32[1,3,256,512]{3,2,1,0:T(8,128)} %param.8) | copy-start | bytes 4718596
  3.1 16.6 %collective-permute-start.1 = (f32[256,512]{1,0:T(8,128)}, f32[256,512]{1,0:T(8,128)S(1)}, u32[]{:S(2)}, u32[]{:S(2)}) collective-permute-start(f32[256,512]{1,0:T(8,128)} %get-tuple-element.59), channel_id=1, source_target_pairs={{96,64},{128,160},{97,65},{129,161},{98,66},{130,162},{99,67},{131... | collective-permute-start | bytes 1572872 | tf_op jit(solution)/shard_map/ppermute | solution.py:148
  3.9 16.6 %collective-permute-start = (f32[256,512]{1,0:T(8,128)}, f32[256,512]{1,0:T(8,128)}, u32[]{:S(2)}, u32[]{:S(2)}) collective-permute-start(f32[256,512]{1,0:T(8,128)} %get-tuple-element.61), channel_id=1, source_target_pairs={{32,0},{160,128},{64,96},{192,224},{33,1},{161,129},{65,97},{193,2... | collective-permute-start | bytes 1572872 | tf_op jit(solution)/shard_map/ppermute | solution.py:148
  9.6 0.7 copy-start.9
  11.2 12.8 %collective-permute-start.5 = (f32[256,512]{1,0:T(8,128)}, f32[256,512]{1,0:T(8,128)}, u32[]{:S(2)}, u32[]{:S(2)}) collective-permute-start(f32[256,512]{1,0:T(8,128)} %fusion.10), channel_id=1, source_target_pairs={{0,16},{31,15},{64,80},{95,79},{128,144},{159,143},{192,208},{223,... | collective-permute-start | bytes 1572872 | tf_op jit(solution)/shard_map/ppermute | solution.py:123
  12.7 12.3 %collective-permute-start.6 = (f32[256,512]{1,0:T(8,128)}, f32[256,512]{1,0:T(8,128)}, u32[]{:S(2)}, u32[]{:S(2)}) collective-permute-start(f32[256,512]{1,0:T(8,128)} %fusion.10), channel_id=1, source_target_pairs={{0,24},{31,7},{64,88},{95,71},{128,152},{159,135},{192,216},{223,1... | collective-permute-start | bytes 1572872 | tf_op jit(solution)/shard_map/ppermute | solution.py:123
  14.0 11.0 %collective-permute-start.4 = (f32[256,512]{1,0:T(8,128)}, f32[256,512]{1,0:T(8,128)}, u32[]{:S(2)}, u32[]{:S(2)}) collective-permute-start(f32[256,512]{1,0:T(8,128)} %fusion.10), channel_id=1, source_target_pairs={{0,8},{31,23},{64,72},{95,87},{128,136},{159,151},{192,200},{223,2... | collective-permute-start | bytes 1572872 | tf_op jit(solution)/shard_map/ppermute | solution.py:123
  19.7 5.3 %copy-start.10 = (f32[256,256]{1,0:T(8,128)S(1)}, f32[256,256]{1,0:T(8,128)}, u32[]{:S(2)}) copy-start(f32[256,256]{1,0:T(8,128)} %copy-done.9) | copy-start | bytes 786436
  19.7 0.8 copy-start.11
  22.5 21.8 %collective-permute-start.2 = (f32[256,512]{1,0:T(8,128)}, f32[256,512]{1,0:T(8,128)}, u32[]{:S(2)}, u32[]{:S(2)}) collective-permute-start(f32[256,512]{1,0:T(8,128)} %get-tuple-element.57), channel_id=1, source_target_pairs={{96,32},{128,192},{97,33},{129,193},{98,34},{130,194},{99,35},{131... | collective-permute-start | bytes 1572872 | tf_op jit(solution)/shard_map/ppermute | solution.py:148
  27.4 20.1 %collective-permute-start.8 = (f32[256,512]{1,0:T(8,128)}, f32[256,512]{1,0:T(8,128)S(1)}, u32[]{:S(2)}, u32[]{:S(2)}) collective-permute-start(f32[256,512]{1,0:T(8,128)} %get-tuple-element.48), channel_id=1, source_target_pairs={{0,2},{8,10},{16,18},{24,26},{7,5},{23,21},{15,13},{31,29},{64,66}... | collective-permute-start | bytes 1572872 | tf_op jit(solution)/shard_map/ppermute | solution.py:123
  35.5 12.0 %collective-permute-start.9 = (f32[256,512]{1,0:T(8,128)}, f32[256,512]{1,0:T(8,128)}, u32[]{:S(2)}, u32[]{:S(2)}) collective-permute-start(f32[256,512]{1,0:T(8,128)} %get-tuple-element.48), channel_id=1, source_target_pairs={{0,3},{8,11},{16,19},{24,27},{7,4},{23,20},{15,12},{31,28},{64,67}... | collective-permute-start | bytes 1572872 | tf_op jit(solution)/shard_map/ppermute | solution.py:123
  37.6 15.5 %collective-permute-start.7 = (f32[256,512]{1,0:T(8,128)}, f32[256,512]{1,0:T(8,128)}, u32[]{:S(2)}, u32[]{:S(2)}) collective-permute-start(f32[256,512]{1,0:T(8,128)} %get-tuple-element.48), channel_id=1, source_target_pairs={{0,1},{8,9},{16,17},{24,25},{7,6},{23,22},{15,14},{31,30},{64,65},... | collective-permute-start | bytes 1572872 | tf_op jit(solution)/shard_map/ppermute | solution.py:123
  45.4 12.9 %collective-permute-start.3 = (f32[256,512]{1,0:T(8,128)S(1)}, f32[256,512]{1,0:T(8,128)}, u32[]{:S(2)}, u32[]{:S(2)}) collective-permute-start(f32[256,512]{1,0:T(8,128)S(1)} %broadcast_select_fusion.8), channel_id=1, source_target_pairs={{96,0},{128,224},{97,1},{129,225},{98,2},{130,226},{99,3},{131,227... | collective-permute-start | bytes 1572872 | tf_op jit(solution)/shard_map/ppermute | solution.py:148
  55.6 9.5 %collective-permute-start.10 = (f32[256,512]{1,0:T(8,128)}, f32[256,512]{1,0:T(8,128)S(1)}, u32[]{:S(2)}, u32[]{:S(2)}) collective-permute-start(f32[256,512]{1,0:T(8,128)} %get-tuple-element.45), channel_id=1, source_target_pairs={{0,4},{1,5},{2,6},{3,7},{8,12},{9,13},{10,14},{11,15},{16,20},{17,... | collective-permute-start | bytes 1572872 | tf_op jit(solution)/shard_map/ppermute | solution.py:123
  67.1 2.1 %collective-permute-start.11 = (f32[256,512]{1,0:T(8,128)}, f32[256,512]{1,0:T(8,128)S(1)}, u32[]{:S(2)}, u32[]{:S(2)}) collective-permute-start(f32[256,512]{1,0:T(8,128)} %broadcast_select_fusion.1), channel_id=1, source_target_pairs={{0,32},{64,96},{128,160},{192,224},{32,0},{96,64},{160,128},{224,1... | collective-permute-start | bytes 1572872 | tf_op jit(solution)/shard_map/ppermute | solution.py:168
  70.1 1.4 %copy-start.7 = (f32[256,256]{1,0:T(8,128)}, f32[256,256]{1,0:T(8,128)S(1)}, u32[]{:S(2)}) copy-start(f32[256,256]{1,0:T(8,128)S(1)} %fusion.11) | copy-start | bytes 786436
  70.5 1.0 copy-start.8
  71.6 1.7 %copy-start.1 = (f32[256,512]{1,0:T(8,128)}, f32[256,512]{1,0:T(8,128)S(1)}, u32[]{:S(2)}) copy-start(f32[256,512]{1,0:T(8,128)S(1)} %fusion.3) | copy-start | bytes 1572868
  72.4 2.3 %copy-start.3 = (f32[256,256]{1,0:T(8,128)}, f32[256,256]{1,0:T(8,128)S(1)}, u32[]{:S(2)}) copy-start(f32[256,256]{1,0:T(8,128)S(1)} %get-tuple-element.69) | copy-start | bytes 786436
  72.4 3.7 %copy-start.5 = (f32[256,256]{1,0:T(8,128)}, f32[256,256]{1,0:T(8,128)S(1)}, u32[]{:S(2)}) copy-start(f32[256,256]{1,0:T(8,128)S(1)} %get-tuple-element.83) | copy-start | bytes 786436
  73.3 14.6 %collective-permute-start.12 = (f32[256,512]{1,0:T(8,128)}, f32[256,512]{1,0:T(8,128)S(1)}, u32[]{:S(2)}, u32[]{:S(2)}) collective-permute-start(f32[256,512]{1,0:T(8,128)} %fusion.9), channel_id=1, source_target_pairs={{32,96},{160,224},{64,0},{192,128},{33,97},{161,225},{65,1},{193,1... | collective-permute-start | bytes 1572872 | tf_op jit(solution)/shard_map/ppermute | solution.py:168
  74.6 13.3 %collective-permute-start.13 = (f32[256,512]{1,0:T(8,128)}, f32[256,512]{1,0:T(8,128)}, u32[]{:S(2)}, u32[]{:S(2)}) collective-permute-start(f32[256,512]{1,0:T(8,128)} %fusion.9), channel_id=1, source_target_pairs={{32,64},{160,192},{64,32},{192,160},{33,65},{161,193},{65,33},{193... | collective-permute-start | bytes 1572872 | tf_op jit(solution)/shard_map/ppermute | solution.py:168
  76.1 11.8 %collective-permute-start.14 = (f32[256,512]{1,0:T(8,128)}, f32[256,512]{1,0:T(8,128)}, u32[]{:S(2)}, u32[]{:S(2)}) collective-permute-start(f32[256,512]{1,0:T(8,128)} %fusion.9), channel_id=1, source_target_pairs={{32,0},{160,128},{64,96},{192,224},{33,1},{161,129},{65,97},{193,2... | collective-permute-start | bytes 1572872 | tf_op jit(solution)/shard_map/ppermute | solution.py:168
  79.4 8.5 %copy-start.4 = (f32[256,256]{1,0:T(8,128)S(1)}, f32[256,256]{1,0:T(8,128)}, u32[]{:S(2)}) copy-start(f32[256,256]{1,0:T(8,128)} %copy-done.3) | copy-start | bytes 786436
  79.4 8.5 %copy-start.6 = (f32[256,256]{1,0:T(8,128)S(1)}, f32[256,256]{1,0:T(8,128)}, u32[]{:S(2)}) copy-start(f32[256,256]{1,0:T(8,128)} %copy-done.5) | copy-start | bytes 786436
  89.3 1.6 %copy-start.2 = (f32[256,512]{1,0:T(8,128)S(1)}, f32[256,512]{1,0:T(8,128)}, u32[]{:S(2)}) copy-start(f32[256,512]{1,0:T(8,128)} %copy-done.1) | copy-start | bytes 1572868
  93.2 11.6 %collective-permute-start.15 = (f32[256,512]{1,0:T(8,128)}, f32[256,512]{1,0:T(8,128)S(1)}, u32[]{:S(2)}, u32[]{:S(2)}) collective-permute-start(f32[256,512]{1,0:T(8,128)} %fusion.8), channel_id=1, source_target_pairs={{96,224},{128,0},{97,225},{129,1},{98,226},{130,2},{99,227},{131,3... | collective-permute-start | bytes 1572872 | tf_op jit(solution)/shard_map/ppermute | solution.py:168
  94.5 11.8 %collective-permute-start.16 = (f32[256,512]{1,0:T(8,128)}, f32[256,512]{1,0:T(8,128)S(1)}, u32[]{:S(2)}, u32[]{:S(2)}) collective-permute-start(f32[256,512]{1,0:T(8,128)} %fusion.8), channel_id=1, source_target_pairs={{96,192},{128,32},{97,193},{129,33},{98,194},{130,34},{99,195},{13... | collective-permute-start | bytes 1572872 | tf_op jit(solution)/shard_map/ppermute | solution.py:168
  95.4 20.0 %collective-permute-start.17 = (f32[256,512]{1,0:T(8,128)}, f32[256,512]{1,0:T(8,128)}, u32[]{:S(2)}, u32[]{:S(2)}) collective-permute-start(f32[256,512]{1,0:T(8,128)} %fusion.8), channel_id=1, source_target_pairs={{96,160},{128,64},{97,161},{129,65},{98,162},{130,66},{99,163},{13... | collective-permute-start | bytes 1572872 | tf_op jit(solution)/shard_map/ppermute | solution.py:168
  96.9 18.5 %collective-permute-start.18 = (f32[256,512]{1,0:T(8,128)}, f32[256,512]{1,0:T(8,128)}, u32[]{:S(2)}, u32[]{:S(2)}) collective-permute-start(f32[256,512]{1,0:T(8,128)} %fusion.8), channel_id=1, source_target_pairs={{96,128},{128,96},{97,129},{129,97},{98,130},{130,98},{99,131},{13... | collective-permute-start | bytes 1572872 | tf_op jit(solution)/shard_map/ppermute | solution.py:168
  98.4 17.0 %collective-permute-start.19 = (f32[256,512]{1,0:T(8,128)}, f32[256,512]{1,0:T(8,128)}, u32[]{:S(2)}, u32[]{:S(2)}) collective-permute-start(f32[256,512]{1,0:T(8,128)} %fusion.8), channel_id=1, source_target_pairs={{96,64},{128,160},{97,65},{129,161},{98,66},{130,162},{99,67},{131... | collective-permute-start | bytes 1572872 | tf_op jit(solution)/shard_map/ppermute | solution.py:168
  104.8 10.6 %collective-permute-start.20 = (f32[256,512]{1,0:T(8,128)}, f32[256,512]{1,0:T(8,128)}, u32[]{:S(2)}, u32[]{:S(2)}) collective-permute-start(f32[256,512]{1,0:T(8,128)} %fusion.8), channel_id=1, source_target_pairs={{96,32},{128,192},{97,33},{129,193},{98,34},{130,194},{99,35},{131... | collective-permute-start | bytes 1572872 | tf_op jit(solution)/shard_map/ppermute | solution.py:168
  106.3 19.9 %collective-permute-start.21 = (f32[256,512]{1,0:T(8,128)}, f32[256,512]{1,0:T(8,128)}, u32[]{:S(2)}, u32[]{:S(2)}) collective-permute-start(f32[256,512]{1,0:T(8,128)} %fusion.8), channel_id=1, source_target_pairs={{96,0},{128,224},{97,1},{129,225},{98,2},{130,226},{99,3},{131,227... | collective-permute-start | bytes 1572872 | tf_op jit(solution)/shard_map/ppermute | solution.py:168

commit v3 on v0

--- a/solution.py
+++ b/solution.py
@@ -178,17 +178,14 @@
         tip_rhs = jnp.concatenate([upper_rows, lower_rows], 0)
         solved = jnp.dot(inverses[level], tip_rhs, precision=precise, preferred_element_type=jnp.float32)
         if level + 1 < LEVELS:
-            bottom_prod = jnp.dot(
-                bottom[:, band:], solved[:, : 2 * band], precision=precise, preferred_element_type=jnp.float32
+            tip = jnp.where(side_low, top, bottom)
+            cols = jnp.concatenate(
+                [solved[:, :band], jnp.where(side_low, solved[:, 2 * band :], solved[:, band : 2 * band])], 1
             )
-            bottom = jnp.concatenate([bottom[:, :band] - bottom_prod[:, :band], -bottom_prod[:, band:]], 1)
-            top_prod = jnp.dot(
-                top[:, band:],
-                jnp.concatenate([solved[:, :band], solved[:, 2 * band :]], 1),
-                precision=precise,
-                preferred_element_type=jnp.float32,
-            )
-            top = jnp.concatenate([top[:, :band] - top_prod[:, :band], -top_prod[:, band:]], 1)
+            tip_prod = jnp.dot(tip[:, band:], cols, precision=precise, preferred_element_type=jnp.float32)
+            tip = jnp.concatenate([tip[:, :band] - tip_prod[:, :band], -tip_prod[:, band:]], 1)
+            top = jnp.where(side_low, tip, top)
+            bottom = jnp.where(side_low, bottom, tip)
         flag = jnp.where(side_low, 1, 0).astype(jnp.int32).reshape(1)
         spike_right, spike_left, load_block = bulk_update(flag, solved, spike_right, spike_left, load_block)
     return (spike_right, spike_left, load_block)

time: 132 us -> 133 us (level)
  local copies, waits for them, and re-layouts: 6.51 us -> 7.99 us
    unnamed x18, local copies, waits for them, and re-layouts: 0.04 us -> 1.51 us
    select_n x3, other arithmetic: 3.46 us -> 2.02 us  [on_device(): upper_tip = jnp.where(place == half - offset, got, upper_tip)]
where the time goes in v3:
time: 133 us; the launch traced here: 132 us
  waiting for transfers between devices  35.7 us (27%)
  starting transfers between devices  34.2 us (26%)
  Pallas kernels  20.8 us (16%)
  other arithmetic  14.8 us (11%)
  between operations  11.7 us (9%)
  local copies, waits for them, and re-layouts  7.99 us (6%)
  matrix products  6.53 us (5%)
    ppermute x11, waiting for transfers between devices, on_device(): got = lax.ppermute(sent, 'chain', pairs)  21.6 us
    pallas_call x3, Pallas kernels, bulk_update(): pl.pallas_call(bulk_kernel, grid_spec=pltpu.PrefetchScalarGridSpec(num_sc...  20.8 us
    ppermute x7, starting transfers between devices, core_tree(): lax.ppermute(sent, ('chain', 'rows'), pairs)  17.6 us
    ppermute x7, waiting for transfers between devices, core_tree(): lax.ppermute(sent, ('chain', 'rows'), pairs)  14.1 us
    ppermute x11, starting transfers between devices, on_device(): got = lax.ppermute(sent, 'chain', pairs)  11.9 us
    select_n x3, other arithmetic, core_tree(): sent = jnp.where(mine[3 * step + 2] == 1, top, bottom)  5.59 us
    dot_general x3, matrix products, on_device(): jnp.dot(inverses[level], tip_rhs, precision=precise, preferred_element_ty...  5.3 us
    ppermute x4, starting transfers between devices, on_device(): got = lax.ppermute(mine, 'chain', pairs)  4.73 us
  transfers between devices with their start and end apart: 22, of which 8 were waited for; matrix products, arithmetic and copies ran while one was open for 10% of the time, Pallas kernels for 11%

profile of v3, /device:TPU:31, one launch (start us, length us, event | category | flops | bytes accessed | tf_op | source)
XLA Modules:
  0.0 131.7 jit_solution(5916221530748807300)
XLA Ops:
  0.6 2.5 %slice_bitcast_fusion = (f32[256,512]{1,0:T(8,128)}, f32[256,512]{1,0:T(8,128)}, f32[256,512]{1,0:T(8,128)}) fusion(f32[1,3,256,512]{3,2,1,0:T(8,128)} %param.8), kind=kLoop, calls=%fused_computation.51 | loop fusion | bytes 3145728 | tf_op jit(solution)/shard_map/squeeze | solution.py:145
  3.2 0.7 collective-permute-start.1
  3.9 1.3 collective-permute-start
  5.2 1.0 slice.136
  6.2 1.1 slice.133
  7.3 0.7 fusion.64
  8.6 1.1 fusion.58
  9.7 0.9 fusion.42
  10.5 1.5 %collective-permute-start.5 = (f32[256,512]{1,0:T(8,128)}, f32[256,512]{1,0:T(8,128)}, u32[]{:S(2)}, u32[]{:S(2)}) collective-permute-start(f32[256,512]{1,0:T(8,128)} %fusion.42), channel_id=1, source_target_pairs={{0,16},{31,15},{64,80},{95,79},{128,144},{159,143},{192,208},{223,... | collective-permute-start | bytes 1572872 | tf_op jit(solution)/shard_map/ppermute | solution.py:123
  12.0 1.3 collective-permute-start.6
  13.3 1.5 %collective-permute-start.4 = (f32[256,512]{1,0:T(8,128)}, f32[256,512]{1,0:T(8,128)}, u32[]{:S(2)}, u32[]{:S(2)}) collective-permute-start(f32[256,512]{1,0:T(8,128)} %fusion.42), channel_id=1, source_target_pairs={{0,8},{31,23},{64,72},{95,87},{128,136},{159,151},{192,200},{223,2... | collective-permute-start | bytes 1572872 | tf_op jit(solution)/shard_map/ppermute | solution.py:123
  19.2 0.8 copy-done.7
  20.0 2.1 %broadcast_select_fusion.11 = (f32[256,512]{1,0:T(8,128)S(1)}, f32[256,512]{1,0:T(8,128)}) fusion(f32[256,512]{1,0:T(8,128)} %copy-done.7, pred[]{:T(512)S(6)} %or.15, f32[1,3,256,512]{3,2,1,0:T(8,128)S(1)} %copy-done, f32[256,512]{1,0:T(8,128)} %collective-permute-done, pred[]{:T(512)S(6)} %or.12), kind=kLoop, calls=%fused_computation.78 | loop fusion | flops 262144 | bytes 3145730 | tf_op jit(solution)/shard_map/jit(_where)/select_n | solution.py:149
  22.0 1.5 %collective-permute-start.2 = (f32[256,512]{1,0:T(8,128)S(1)}, f32[256,512]{1,0:T(8,128)}, u32[]{:S(2)}, u32[]{:S(2)}) collective-permute-start(f32[256,512]{1,0:T(8,128)S(1)} %get-tuple-element.58), channel_id=1, source_target_pairs={{96,32},{128,192},{97,33},{129,193},{98,34},{130,194},{99,35},{131... | collective-permute-start | bytes 1572872 | tf_op jit(solution)/shard_map/ppermute | solution.py:148
  23.5 0.7 collective-permute-done.6
  24.2 2.4 %broadcast_select_fusion.9 = (f32[256,512]{1,0:T(8,128)}, f32[256,512]{1,0:T(8,128)S(1)}, f32[256,512]{1,0:T(8,128)S(1)}) fusion(pred[]{:T(512)} %bitcast.11, f32[256,512]{1,0:T(8,128)} %collective-permute-done.5, f32[256,512]{1,0:T(8,128)} %collective-permute-done.6, pred[]{:T(512)} %bitcast.14, f32[256,512]{1,0:T(8,128)} %collective-permute-done.4, ...), kind=kLoop, calls=%fused_computation.76 | loop fusion | flops 1179648 | bytes 4194311 | tf_op jit(solution)/shard_map/jit(_where)/select_n | solution.py:122
  26.7 8.3 %collective-permute-start.8 = (f32[256,512]{1,0:T(8,128)}, f32[256,512]{1,0:T(8,128)S(1)}, u32[]{:S(2)}, u32[]{:S(2)}) collective-permute-start(f32[256,512]{1,0:T(8,128)} %get-tuple-element.51), channel_id=1, source_target_pairs={{0,2},{8,10},{16,18},{24,26},{7,5},{23,21},{15,13},{31,29},{64,66}... | collective-permute-start | bytes 1572872 | tf_op jit(solution)/shard_map/ppermute | solution.py:123
  34.9 1.3 %collective-permute-start.9 = (f32[256,512]{1,0:T(8,128)}, f32[256,512]{1,0:T(8,128)S(1)}, u32[]{:S(2)}, u32[]{:S(2)}) collective-permute-start(f32[256,512]{1,0:T(8,128)} %get-tuple-element.51), channel_id=1, source_target_pairs={{0,3},{8,11},{16,19},{24,27},{7,4},{23,20},{15,12},{31,28},{64,67}... | collective-permute-start | bytes 1572872 | tf_op jit(solution)/shard_map/ppermute | solution.py:123
  36.3 2.1 %collective-permute-start.7 = (f32[256,512]{1,0:T(8,128)}, f32[256,512]{1,0:T(8,128)}, u32[]{:S(2)}, u32[]{:S(2)}) collective-permute-start(f32[256,512]{1,0:T(8,128)} %get-tuple-element.51), channel_id=1, source_target_pairs={{0,1},{8,9},{16,17},{24,25},{7,6},{23,22},{15,14},{31,30},{64,65},... | collective-permute-start | bytes 1572872 | tf_op jit(solution)/shard_map/ppermute | solution.py:123
  42.7 0.1 broadcast_select_fusion.12
  42.8 1.3 collective-permute-start.3
  44.1 2.9 %collective-permute-done.8 = f32[256,512]{1,0:T(8,128)S(1)} collective-permute-done((f32[256,512]{1,0:T(8,128)}, f32[256,512]{1,0:T(8,128)S(1)}, u32[]{:S(2)}, u32[]{:S(2)}) %collective-permute-start.8) | collective-permute-done | bytes 524320 | tf_op jit(solution)/shard_map/ppermute | solution.py:123
  46.9 5.9 %collective-permute-done.7 = f32[256,512]{1,0:T(8,128)} collective-permute-done((f32[256,512]{1,0:T(8,128)}, f32[256,512]{1,0:T(8,128)}, u32[]{:S(2)}, u32[]{:S(2)}) %collective-permute-start.7) | collective-permute-done | bytes 524320 | tf_op jit(solution)/shard_map/ppermute | solution.py:123
  52.8 2.3 %broadcast_select_fusion.8 = (f32[256,512]{1,0:T(8,128)}, f32[256,512]{1,0:T(8,128)S(1)}, f32[256,512]{1,0:T(8,128)S(1)}) fusion(pred[]{:T(512)} %bitcast.16, f32[256,512]{1,0:T(8,128)S(1)} %collective-permute-done.8, f32[256,512]{1,0:T(8,128)} %copy-done.3, pred[]{:T(512)} %bitcast.19, f32[256,512]{1,0:T(8,128)S(1)} %get-tuple-element.52, ...), kind=kLoop, calls=%fused_computation.75 | loop fusion | flops 917504 | bytes 4194311 | tf_op jit(solution)/shard_map/jit(_where)/select_n | solution.py:122
  55.1 1.7 %collective-permute-start.10 = (f32[256,512]{1,0:T(8,128)}, f32[256,512]{1,0:T(8,128)S(1)}, u32[]{:S(2)}, u32[]{:S(2)}) collective-permute-start(f32[256,512]{1,0:T(8,128)} %get-tuple-element.48), channel_id=1, source_target_pairs={{0,4},{1,5},{2,6},{3,7},{8,12},{9,13},{10,14},{11,15},{16,20},{17,... | collective-permute-start | bytes 1572872 | tf_op jit(solution)/shard_map/ppermute | solution.py:123
  58.1 2.0 %broadcast_select_fusion.13 = f32[256,512]{1,0:T(8,128)} fusion(f32[256,512]{1,0:T(8,128)} %collective-permute-done.3, f32[256,512]{1,0:T(8,128)S(1)} %broadcast_select_fusion.12, pred[]{:T(512)S(6)} %or.13), kind=kLoop, calls=%fused_computation.80 | loop fusion | flops 131072 | bytes 1572865 | tf_op jit(solution)/shard_map/jit(_where)/select_n | solution.py:149
  60.0 4.6 %collective-permute-done.10 = f32[256,512]{1,0:T(8,128)S(1)} collective-permute-done((f32[256,512]{1,0:T(8,128)}, f32[256,512]{1,0:T(8,128)S(1)}, u32[]{:S(2)}, u32[]{:S(2)}) %collective-permute-start.10) | collective-permute-done | bytes 524320 | tf_op jit(solution)/shard_map/ppermute | solution.py:123
  64.6 0.1 broadcast_select_fusion.7
  64.7 0.1 broadcast_select_fusion.4
  64.9 0.1 collective-permute-start.11
  65.0 1.9 %collective-permute-done.11 = f32[256,512]{1,0:T(8,128)S(1)} collective-permute-done((f32[256,512]{1,0:T(8,128)S(1)}, f32[256,512]{1,0:T(8,128)S(1)}, u32[]{:S(2)}, u32[]{:S(2)}) %collective-permute-start.11) | collective-permute-done | bytes 524320 | tf_op jit(solution)/shard_map/ppermute | solution.py:169
  66.9 0.1 broadcast_select_fusion.1
  67.1 1.5 %fusion.2.x_ref = f32[256,768]{1,0:T(8,128)S(1)} fusion(f32[256,512]{1,0:T(8,128)S(1)} %copy-done.5, f32[256,256]{1,0:T(8,128)S(1)} %broadcast_in_dim.3, f32[256,512]{1,0:T(8,128)S(1)} %get-tuple-element.80, f32[256,256]{1,0:T(8,128)S(1)} %get-tuple-element.78, f32[256,256]{1,0:T(8,128)S(1)} %get-tuple-element.77), kind=kOutput, calls=%fused_computation.5 | convolution fusion | flops 1209925632 | bytes 2621440 | tf_op jit(solution)/shard_map/dot_general | solution.py:179
  68.7 0.6 fusion.30
  69.3 0.1 slice_subtract_fusion.1
  69.3 0.1 copy-done.2
  69.5 0.2 broadcast_select_fusion.5
  69.7 0.9 broadcast_select_fusion
  70.6 1.3 collective-permute-start.12
  71.9 0.7 collective-permute-start.13
  72.6 1.3 collective-permute-start.14
  73.9 6.9 %shard_map.76 = (f32[2048,256]{1,0:T(8,128)}, f32[2048,256]{1,0:T(8,128)}, f32[2048,256]{1,0:T(8,128)}) custom-call(s32[1]{0:T(128)} %bitcast.21.flag_ref, f32[256,768]{1,0:T(8,128)} %copy-done.2, f32[2048,256]{1,0:T(8,128)} %v_ref.1, f32[2048,256]{1,0:T(8,128)} %w_ref.1, f32[2048,256]{1,0:T(8,128)} %g_ref.1), custom_call_target="tpu_custom_call" | custom-call | tf_op jit(solution)/shard_map/pallas_call | solution.py:67
  80.8 3.5 %collective-permute-done.12 = f32[256,512]{1,0:T(8,128)S(1)} collective-permute-done((f32[256,512]{1,0:T(8,128)}, f32[256,512]{1,0:T(8,128)S(1)}, u32[]{:S(2)}, u32[]{:S(2)}) %collective-permute-start.12) | collective-permute-done | bytes 524320 | tf_op jit(solution)/shard_map/ppermute | solution.py:169
  84.4 0.3 select_select_fusion.2
  84.7 1.5 %fusion.6.x_ref = f32[256,768]{1,0:T(8,128)S(1)} fusion(f32[256,512]{1,0:T(8,128)S(1)} %copy-done.6, f32[256,256]{1,0:T(8,128)S(1)} %broadcast_in_dim.3, f32[256,512]{1,0:T(8,128)S(1)} %get-tuple-element.32, f32[256,256]{1,0:T(8,128)S(1)} %get-tuple-element.74, f32[256,256]{1,0:T(8,128)S(1)} %get-tuple-element.73), kind=kOutput, calls=%fused_computation.8 | convolution fusion | flops 1209925632 | bytes 2621440 | tf_op jit(solution)/shard_map/dot_general | solution.py:179
  86.3 0.6 fusion.34
  86.9 0.1 slice_subtract_fusion
  87.0 0.1 copy-done.1
  87.1 1.0 broadcast_select_fusion.6
  88.1 1.3 collective-permute-start.15
  89.4 0.7 collective-permute-start.16
  90.1 0.7 collective-permute-start.17
  90.8 1.5 %collective-permute-start.18 = (f32[256,512]{1,0:T(8,128)}, f32[256,512]{1,0:T(8,128)}, u32[]{:S(2)}, u32[]{:S(2)}) collective-permute-start(f32[256,512]{1,0:T(8,128)} %broadcast_select_fusion.6), channel_id=1, source_target_pairs={{96,128},{128,96},{97,129},{129,97},{98,130},{130,98},{99,131},{13... | collective-permute-start | bytes 1572872 | tf_op jit(solution)/shard_map/ppermute | solution.py:169
  92.3 1.5 %collective-permute-start.19 = (f32[256,512]{1,0:T(8,128)}, f32[256,512]{1,0:T(8,128)}, u32[]{:S(2)}, u32[]{:S(2)}) collective-permute-start(f32[256,512]{1,0:T(8,128)} %broadcast_select_fusion.6), channel_id=1, source_target_pairs={{96,64},{128,160},{97,65},{129,161},{98,66},{130,162},{99,67},{131... | collective-permute-start | bytes 1572872 | tf_op jit(solution)/shard_map/ppermute | solution.py:169
  93.8 6.0 %collective-permute-done.15 = f32[256,512]{1,0:T(8,128)S(1)} collective-permute-done((f32[256,512]{1,0:T(8,128)}, f32[256,512]{1,0:T(8,128)S(1)}, u32[]{:S(2)}, u32[]{:S(2)}) %collective-permute-start.15) | collective-permute-done | bytes 524320 | tf_op jit(solution)/shard_map/ppermute | solution.py:169
  99.7 1.4 %collective-permute-start.20 = (f32[256,512]{1,0:T(8,128)}, f32[256,512]{1,0:T(8,128)}, u32[]{:S(2)}, u32[]{:S(2)}) collective-permute-start(f32[256,512]{1,0:T(8,128)} %broadcast_select_fusion.6), channel_id=1, source_target_pairs={{96,32},{128,192},{97,33},{129,193},{98,34},{130,194},{99,35},{131... | collective-permute-start | bytes 1572872 | tf_op jit(solution)/shard_map/ppermute | solution.py:169
  101.2 1.5 %collective-permute-start.21 = (f32[256,512]{1,0:T(8,128)}, f32[256,512]{1,0:T(8,128)}, u32[]{:S(2)}, u32[]{:S(2)}) collective-permute-start(f32[256,512]{1,0:T(8,128)} %broadcast_select_fusion.6), channel_id=1, source_target_pairs={{96,0},{128,224},{97,1},{129,225},{98,2},{130,226},{99,3},{131,227... | collective-permute-start | bytes 1572872 | tf_op jit(solution)/shard_map/ppermute | solution.py:169
  102.6 6.9 %shard_map.77 = (f32[2048,256]{1,0:T(8,128)}, f32[2048,256]{1,0:T(8,128)}, f32[2048,256]{1,0:T(8,128)}) custom-call(s32[1]{0:T(128)} %bitcast.22.flag_ref, f32[256,768]{1,0:T(8,128)} %copy-done.1, f32[2048,256]{1,0:T(8,128)} %get-tuple-element.34.v_ref, f32[2048,256]{1,0:T(8,128)} %get-tuple-element.35.w_ref, f32[2048,256]{1,0:T(8,128)} %get-tuple-element.36.g_ref), custom_call_target="tpu_custom_call" | custom-call | tf_op jit(solution)/shard_map/pallas_call | solution.py:67
  109.6 10.2 %collective-permute-done.21 = f32[256,512]{1,0:T(8,128)} collective-permute-done((f32[256,512]{1,0:T(8,128)}, f32[256,512]{1,0:T(8,128)}, u32[]{:S(2)}, u32[]{:S(2)}) %collective-permute-start.21) | collective-permute-done | bytes 524320 | tf_op jit(solution)/shard_map/ppermute | solution.py:169
  119.8 1.6 %select_select_fusion = f32[256,512]{1,0:T(8,128)S(1)} fusion(f32[256,512]{1,0:T(8,128)S(1)} %collective-permute-done.15, f32[256,512]{1,0:T(8,128)S(1)} %collective-permute-done.16, f32[256,512]{1,0:T(8,128)S(1)} %collective-permute-done.17, f32[256,512]{1,0:T(8,128)} %collective-permute-done.18, f32[256,512]{1,0:T(8,128)} %collective-permute-done.19, ...), kind=kLoop, calls=%fused_computation.43 | loop fusion | flops 1179648 | bytes 5242888 | tf_op jit(solution)/shard_map/jit(_where)/select_n | solution.py:171
  121.4 0.6 select_select_fusion.1
  122.0 0.4 copy-done.4
  122.5 2.3 %fusion.10.x_ref = f32[256,768]{1,0:T(8,128)} fusion(f32[256,512]{1,0:T(8,128)S(1)} %copy-done.4, f32[256,256]{1,0:T(8,128)S(1)} %broadcast_in_dim.3, f32[256,512]{1,0:T(8,128)S(1)} %select_select_fusion.1, f32[256,256]{1,0:T(8,128)S(1)} %get-tuple-element.70, f32[256,256]{1,0:T(8,128)S(1)} %get-tuple-element.69), kind=kOutput, calls=%fused_computation.11 | convolution fusion | flops 1209925632 | bytes 2621440 | tf_op jit(solution)/shard_map/dot_general | solution.py:179
  124.8 6.9 %shard_map.78 = (f32[2048,256]{1,0:T(8,128)}, f32[2048,256]{1,0:T(8,128)}, f32[2048,256]{1,0:T(8,128)}) custom-call(s32[1]{0:T(128)} %bitcast.flag_ref, f32[256,768]{1,0:T(8,128)} %fusion.10.x_ref, f32[2048,256]{1,0:T(8,128)} %get-tuple-element.42.v_ref, f32[2048,256]{1,0:T(8,128)} %get-tuple-element.43.w_ref, f32[2048,256]{1,0:T(8,128)} %get-tuple-element.44.g_ref), custom_call_target="tpu_custom_call" | custom-call | tf_op jit(solution)/shard_map/pallas_call | solution.py:67
  (34 shorter events, 0.3 us)
Async XLA Ops:
  0.6 6.6 %copy-start.8 = (s32[9,2,32]{2,1,0:T(2,128)S(1)}, s32[9,2,32]{2,1,0:T(2,128)}, u32[]{:S(2)}) copy-start(s32[9,2,32]{2,1,0:T(2,128)} %constant.82.clone) | copy-start | bytes 6916
  3.2 16.0 %collective-permute-start.1 = (f32[256,512]{1,0:T(8,128)}, f32[256,512]{1,0:T(8,128)S(1)}, u32[]{:S(2)}, u32[]{:S(2)}) collective-permute-start(f32[256,512]{1,0:T(8,128)} %get-tuple-element.60), channel_id=1, source_target_pairs={{96,64},{128,160},{97,65},{129,161},{98,66},{130,162},{99,67},{131... | collective-permute-start | bytes 1572872 | tf_op jit(solution)/shard_map/ppermute | solution.py:148
  3.9 16.1 %collective-permute-start = (f32[256,512]{1,0:T(8,128)}, f32[256,512]{1,0:T(8,128)}, u32[]{:S(2)}, u32[]{:S(2)}) collective-permute-start(f32[256,512]{1,0:T(8,128)} %get-tuple-element.62), channel_id=1, source_target_pairs={{32,0},{160,128},{64,96},{192,224},{33,1},{161,129},{65,97},{193,2... | collective-permute-start | bytes 1572872 | tf_op jit(solution)/shard_map/ppermute | solution.py:148
  6.2 13.8 %copy-start = (f32[1,3,256,512]{3,2,1,0:T(8,128)S(1)}, f32[1,3,256,512]{3,2,1,0:T(8,128)}, u32[]{:S(2)}) copy-start(f32[1,3,256,512]{3,2,1,0:T(8,128)} %param.8) | copy-start | bytes 4718596
  10.5 13.0 %collective-permute-start.5 = (f32[256,512]{1,0:T(8,128)}, f32[256,512]{1,0:T(8,128)}, u32[]{:S(2)}, u32[]{:S(2)}) collective-permute-start(f32[256,512]{1,0:T(8,128)} %fusion.42), channel_id=1, source_target_pairs={{0,16},{31,15},{64,80},{95,79},{128,144},{159,143},{192,208},{223,... | collective-permute-start | bytes 1572872 | tf_op jit(solution)/shard_map/ppermute | solution.py:123
  12.0 12.2 %collective-permute-start.6 = (f32[256,512]{1,0:T(8,128)}, f32[256,512]{1,0:T(8,128)}, u32[]{:S(2)}, u32[]{:S(2)}) collective-permute-start(f32[256,512]{1,0:T(8,128)} %fusion.42), channel_id=1, source_target_pairs={{0,24},{31,7},{64,88},{95,71},{128,152},{159,135},{192,216},{223,1... | collective-permute-start | bytes 1572872 | tf_op jit(solution)/shard_map/ppermute | solution.py:123
  13.3 11.0 %collective-permute-start.4 = (f32[256,512]{1,0:T(8,128)}, f32[256,512]{1,0:T(8,128)}, u32[]{:S(2)}, u32[]{:S(2)}) collective-permute-start(f32[256,512]{1,0:T(8,128)} %fusion.42), channel_id=1, source_target_pairs={{0,8},{31,23},{64,72},{95,87},{128,136},{159,151},{192,200},{223,2... | collective-permute-start | bytes 1572872 | tf_op jit(solution)/shard_map/ppermute | solution.py:123
  19.2 0.8 copy-start.7
  22.0 20.6 %collective-permute-start.2 = (f32[256,512]{1,0:T(8,128)S(1)}, f32[256,512]{1,0:T(8,128)}, u32[]{:S(2)}, u32[]{:S(2)}) collective-permute-start(f32[256,512]{1,0:T(8,128)S(1)} %get-tuple-element.58), channel_id=1, source_target_pairs={{96,32},{128,192},{97,33},{129,193},{98,34},{130,194},{99,35},{131... | collective-permute-start | bytes 1572872 | tf_op jit(solution)/shard_map/ppermute | solution.py:148
  26.7 20.3 %collective-permute-start.8 = (f32[256,512]{1,0:T(8,128)}, f32[256,512]{1,0:T(8,128)S(1)}, u32[]{:S(2)}, u32[]{:S(2)}) collective-permute-start(f32[256,512]{1,0:T(8,128)} %get-tuple-element.51), channel_id=1, source_target_pairs={{0,2},{8,10},{16,18},{24,26},{7,5},{23,21},{15,13},{31,29},{64,66}... | collective-permute-start | bytes 1572872 | tf_op jit(solution)/shard_map/ppermute | solution.py:123
  34.9 12.0 %collective-permute-start.9 = (f32[256,512]{1,0:T(8,128)}, f32[256,512]{1,0:T(8,128)S(1)}, u32[]{:S(2)}, u32[]{:S(2)}) collective-permute-start(f32[256,512]{1,0:T(8,128)} %get-tuple-element.51), channel_id=1, source_target_pairs={{0,3},{8,11},{16,19},{24,27},{7,4},{23,20},{15,12},{31,28},{64,67}... | collective-permute-start | bytes 1572872 | tf_op jit(solution)/shard_map/ppermute | solution.py:123
  36.3 16.6 %collective-permute-start.7 = (f32[256,512]{1,0:T(8,128)}, f32[256,512]{1,0:T(8,128)}, u32[]{:S(2)}, u32[]{:S(2)}) collective-permute-start(f32[256,512]{1,0:T(8,128)} %get-tuple-element.51), channel_id=1, source_target_pairs={{0,1},{8,9},{16,17},{24,25},{7,6},{23,22},{15,14},{31,30},{64,65},... | collective-permute-start | bytes 1572872 | tf_op jit(solution)/shard_map/ppermute | solution.py:123
  42.8 15.3 %collective-permute-start.3 = (f32[256,512]{1,0:T(8,128)S(1)}, f32[256,512]{1,0:T(8,128)}, u32[]{:S(2)}, u32[]{:S(2)}) collective-permute-start(f32[256,512]{1,0:T(8,128)S(1)} %broadcast_select_fusion.12), channel_id=1, source_target_pairs={{96,0},{128,224},{97,1},{129,225},{98,2},{130,226},{99,3},{131,227... | collective-permute-start | bytes 1572872 | tf_op jit(solution)/shard_map/ppermute | solution.py:148
  46.9 5.9 %copy-start.3 = (f32[256,512]{1,0:T(8,128)}, f32[256,512]{1,0:T(8,128)S(1)}, u32[]{:S(2)}) copy-start(f32[256,512]{1,0:T(8,128)S(1)} %collective-permute-done.9) | copy-start | bytes 1572868
  55.1 9.5 %collective-permute-start.10 = (f32[256,512]{1,0:T(8,128)}, f32[256,512]{1,0:T(8,128)S(1)}, u32[]{:S(2)}, u32[]{:S(2)}) collective-permute-start(f32[256,512]{1,0:T(8,128)} %get-tuple-element.48), channel_id=1, source_target_pairs={{0,4},{1,5},{2,6},{3,7},{8,12},{9,13},{10,14},{11,15},{16,20},{17,... | collective-permute-start | bytes 1572872 | tf_op jit(solution)/shard_map/ppermute | solution.py:123
  64.9 2.0 %collective-permute-start.11 = (f32[256,512]{1,0:T(8,128)S(1)}, f32[256,512]{1,0:T(8,128)S(1)}, u32[]{:S(2)}, u32[]{:S(2)}) collective-permute-start(f32[256,512]{1,0:T(8,128)S(1)} %get-tuple-element.64), channel_id=1, source_target_pairs={{0,32},{64,96},{128,160},{192,224},{32,0},{96,64},{160,128},{224,1... | collective-permute-start | bytes 1572872 | tf_op jit(solution)/shard_map/ppermute | solution.py:169
  65.0 2.1 %copy-start.5 = (f32[256,512]{1,0:T(8,128)S(1)}, f32[256,512]{1,0:T(8,128)}, u32[]{:S(2)}) copy-start(f32[256,512]{1,0:T(8,128)} %get-tuple-element.27) | copy-start | bytes 1572868
  68.6 0.9 copy-start.2
  70.6 13.8 %collective-permute-start.12 = (f32[256,512]{1,0:T(8,128)}, f32[256,512]{1,0:T(8,128)S(1)}, u32[]{:S(2)}, u32[]{:S(2)}) collective-permute-start(f32[256,512]{1,0:T(8,128)} %broadcast_select_fusion), channel_id=1, source_target_pairs={{32,96},{160,224},{64,0},{192,128},{33,97},{161,225},{65,1},{193,1... | collective-permute-start | bytes 1572872 | tf_op jit(solution)/shard_map/ppermute | solution.py:169
  71.9 12.5 %collective-permute-start.13 = (f32[256,512]{1,0:T(8,128)}, f32[256,512]{1,0:T(8,128)S(1)}, u32[]{:S(2)}, u32[]{:S(2)}) collective-permute-start(f32[256,512]{1,0:T(8,128)} %broadcast_select_fusion), channel_id=1, source_target_pairs={{32,64},{160,192},{64,32},{192,160},{33,65},{161,193},{65,33},{193... | collective-permute-start | bytes 1572872 | tf_op jit(solution)/shard_map/ppermute | solution.py:169
  72.6 11.8 %collective-permute-start.14 = (f32[256,512]{1,0:T(8,128)}, f32[256,512]{1,0:T(8,128)S(1)}, u32[]{:S(2)}, u32[]{:S(2)}) collective-permute-start(f32[256,512]{1,0:T(8,128)} %broadcast_select_fusion), channel_id=1, source_target_pairs={{32,0},{160,128},{64,96},{192,224},{33,1},{161,129},{65,97},{193,2... | collective-permute-start | bytes 1572872 | tf_op jit(solution)/shard_map/ppermute | solution.py:169
  80.8 3.9 %copy-start.6 = (f32[256,512]{1,0:T(8,128)S(1)}, f32[256,512]{1,0:T(8,128)}, u32[]{:S(2)}) copy-start(f32[256,512]{1,0:T(8,128)} %get-tuple-element.28) | copy-start | bytes 1572868
  86.2 0.9 copy-start.1
  88.1 11.6 %collective-permute-start.15 = (f32[256,512]{1,0:T(8,128)}, f32[256,512]{1,0:T(8,128)S(1)}, u32[]{:S(2)}, u32[]{:S(2)}) collective-permute-start(f32[256,512]{1,0:T(8,128)} %broadcast_select_fusion.6), channel_id=1, source_target_pairs={{96,224},{128,0},{97,225},{129,1},{98,226},{130,2},{99,227},{131,3... | collective-permute-start | bytes 1572872 | tf_op jit(solution)/shard_map/ppermute | solution.py:169
  89.4 11.8 %collective-permute-start.16 = (f32[256,512]{1,0:T(8,128)}, f32[256,512]{1,0:T(8,128)S(1)}, u32[]{:S(2)}, u32[]{:S(2)}) collective-permute-start(f32[256,512]{1,0:T(8,128)} %broadcast_select_fusion.6), channel_id=1, source_target_pairs={{96,192},{128,32},{97,193},{129,33},{98,194},{130,34},{99,195},{13... | collective-permute-start | bytes 1572872 | tf_op jit(solution)/shard_map/ppermute | solution.py:169
  90.1 19.5 %collective-permute-start.17 = (f32[256,512]{1,0:T(8,128)}, f32[256,512]{1,0:T(8,128)S(1)}, u32[]{:S(2)}, u32[]{:S(2)}) collective-permute-start(f32[256,512]{1,0:T(8,128)} %broadcast_select_fusion.6), channel_id=1, source_target_pairs={{96,160},{128,64},{97,161},{129,65},{98,162},{130,66},{99,163},{13... | collective-permute-start | bytes 1572872 | tf_op jit(solution)/shard_map/ppermute | solution.py:169
  90.8 18.8 %collective-permute-start.18 = (f32[256,512]{1,0:T(8,128)}, f32[256,512]{1,0:T(8,128)}, u32[]{:S(2)}, u32[]{:S(2)}) collective-permute-start(f32[256,512]{1,0:T(8,128)} %broadcast_select_fusion.6), channel_id=1, source_target_pairs={{96,128},{128,96},{97,129},{129,97},{98,130},{130,98},{99,131},{13... | collective-permute-start | bytes 1572872 | tf_op jit(solution)/shard_map/ppermute | solution.py:169
  92.3 17.3 %collective-permute-start.19 = (f32[256,512]{1,0:T(8,128)}, f32[256,512]{1,0:T(8,128)}, u32[]{:S(2)}, u32[]{:S(2)}) collective-permute-start(f32[256,512]{1,0:T(8,128)} %broadcast_select_fusion.6), channel_id=1, source_target_pairs={{96,64},{128,160},{97,65},{129,161},{98,66},{130,162},{99,67},{131... | collective-permute-start | bytes 1572872 | tf_op jit(solution)/shard_map/ppermute | solution.py:169
  99.7 9.9 %collective-permute-start.20 = (f32[256,512]{1,0:T(8,128)}, f32[256,512]{1,0:T(8,128)}, u32[]{:S(2)}, u32[]{:S(2)}) collective-permute-start(f32[256,512]{1,0:T(8,128)} %broadcast_select_fusion.6), channel_id=1, source_target_pairs={{96,32},{128,192},{97,33},{129,193},{98,34},{130,194},{99,35},{131... | collective-permute-start | bytes 1572872 | tf_op jit(solution)/shard_map/ppermute | solution.py:169
  101.2 18.7 %collective-permute-start.21 = (f32[256,512]{1,0:T(8,128)}, f32[256,512]{1,0:T(8,128)}, u32[]{:S(2)}, u32[]{:S(2)}) collective-permute-start(f32[256,512]{1,0:T(8,128)} %broadcast_select_fusion.6), channel_id=1, source_target_pairs={{96,0},{128,224},{97,1},{129,225},{98,2},{130,226},{99,3},{131,227... | collective-permute-start | bytes 1572872 | tf_op jit(solution)/shard_map/ppermute | solution.py:169
  121.4 1.0 copy-start.4
